TPU v7x, 128 devices: a whole 4x4x4 slice. The times are simulated.
128 devices in a mesh: dp: 16 (over z, x), tensor: 4 (over y), section: 2 (over core).
Axes of the slice: x: 4, y: 4, z: 4, core: 2. Of those that a mesh axis runs over, the one named last changes fastest.
Arguments:
- grad_mat: bfloat16 [16, 4, 1600, 4800], P('dp', 'tensor', 'section'), may hold values from -6 to 6
- grad_vec: bfloat16 [16, 20800], P('dp'), may hold values from -6 to 6
- master_mat: float32 [4, 2, 16, 50, 4800], P('tensor', 'section', 'dp'), may hold values from -9 to 9
- first_mat: float32 [4, 2, 16, 50, 4800], P('tensor', 'section', 'dp'), may hold values from -4 to 4
- second_mat: float32 [4, 2, 16, 50, 4800], P('tensor', 'section', 'dp'), may hold values from 0.001 to 0.1
- master_vec: float32 [16, 1300], P('dp'), may hold values from -6 to 6
- first_vec: float32 [16, 1300], P('dp'), may hold values from -4 to 4
- second_vec: float32 [16, 1300], P('dp'), may hold values from 0.001 to 0.1
Outputs:
- weights_mat: bfloat16 [4, 1600, 4800], P('tensor', 'section')
- weights_vec: bfloat16 [20800], replicated
- new_master_mat: float32 [4, 2, 16, 50, 4800], P('tensor', 'section', 'dp')
- new_first_mat: float32 [4, 2, 16, 50, 4800], P('tensor', 'section', 'dp')
- new_second_mat: float32 [4, 2, 16, 50, 4800], P('tensor', 'section', 'dp')
- new_master_vec: float32 [16, 1300], P('dp')
- new_first_vec: float32 [16, 1300], P('dp')
- new_second_vec: float32 [16, 1300], P('dp')
All inputs are finite; a program needn't handle non-finite values.
Results may differ from a plain program's by a relative error of at most 0.0004.
Values may be sent and summed in bfloat16 or wider, within the bound.
No kernel may reach another device: no remote copies, remote signals or barrier semaphores. Data moves between devices by JAX's collectives and lax.ppermute only.
A program may use at most 128 MiB of HBM per device.

v0:
```python
import jax
import jax.numpy as jnp
from jax import lax
from jax.sharding import PartitionSpec as P

D = 1600
FF = 6400
STEP = 10


BETA_ONE = 0.9
BETA_TWO = 0.999
EPSILON = 1e-06
LEARN_RATE = 0.25
DECAY_MAT = 0.01


def adam_direction(gradient, master, first, second, decay):
    first_new = BETA_ONE * first + (1.0 - BETA_ONE) * gradient
    second_new = BETA_TWO * second + (1.0 - BETA_TWO) * gradient * gradient
    corr_one = 1.0 - BETA_ONE**STEP
    corr_two = 1.0 - BETA_TWO**STEP
    direction = first_new / corr_one / (jnp.sqrt(second_new / corr_two) + EPSILON) + decay * master
    return (first_new, second_new, direction)


def segment_masks(position, bounds):
    lower = jnp.array(bounds[:-1], dtype=jnp.int32)[:, None]
    upper = jnp.array(bounds[1:], dtype=jnp.int32)[:, None]
    return ((position[None, :] >= lower) & (position[None, :] < upper)).astype(jnp.float32)


def local(grad_mat, grad_vec, master_mat, first_mat, second_mat, master_vec, first_vec, second_vec):
    tensor_count = lax.axis_size("tensor")
    section_rows = grad_mat.shape[2]
    columns = grad_mat.shape[3]
    vec_length = grad_vec.shape[1]
    state_shape = master_mat.shape
    vec_shape = master_vec.shape
    owned_vec = vec_shape[1]
    master = master_mat.reshape(-1, columns)
    master_v = master_vec.reshape(owned_vec)
    bounds_mat = [
        0,
        3 * D // tensor_count,
        4 * D // tensor_count,
        (4 * D + FF) // tensor_count,
        columns,
    ]
    masks_mat = segment_masks(lax.iota(jnp.int32, columns), bounds_mat)
    bounds_vec = [0, D, 2 * D, 5 * D, 6 * D, 7 * D, 8 * D, 8 * D + FF, 9 * D + FF]
    vec_index = lax.axis_index("dp") * owned_vec + lax.iota(jnp.int32, owned_vec)
    masks_vec = segment_masks(vec_index, bounds_vec)
    weight_mat_sq = jnp.sum(masks_mat * jnp.sum(master * master, axis=0)[None, :], axis=1)
    weight_vec_sq = jnp.sum(masks_vec * (master_v * master_v)[None, :], axis=1)
    local_grad = grad_mat.reshape(section_rows, columns).astype(jnp.float32)
    local_vec = grad_vec.reshape(vec_length).astype(jnp.float32)
    gradient, gradient_v = (
        lax.psum_scatter(local_grad, "dp", scatter_dimension=0, tiled=True),
        lax.psum_scatter(local_vec, "dp", scatter_dimension=0, tiled=True),
    )
    first_new, second_new, direction = adam_direction(
        gradient, master, first_mat.reshape(-1, columns), second_mat.reshape(-1, columns), DECAY_MAT
    )
    first_v, second_v, direction_v = adam_direction(
        gradient_v, master_v, first_vec.reshape(owned_vec), second_vec.reshape(owned_vec), 0.0
    )
    update_mat_sq = jnp.sum(masks_mat * jnp.sum(direction * direction, axis=0)[None, :], axis=1)
    update_vec_sq = jnp.sum(masks_vec * (direction_v * direction_v)[None, :], axis=1)
    wsum_mat, usum_mat = lax.psum((weight_mat_sq, update_mat_sq), ("dp", "tensor", "section"))
    wsum_vec, usum_vec = lax.psum((weight_vec_sq, update_vec_sq), "dp")
    ratio_mat = jnp.sqrt(wsum_mat) / jnp.sqrt(usum_mat)
    ratio_vec = jnp.sqrt(wsum_vec) / jnp.sqrt(usum_vec)
    ratio_cols = jnp.sum(masks_mat * ratio_mat[:, None], axis=0)
    ratio_entries = jnp.sum(masks_vec * ratio_vec[:, None], axis=0)
    master_new = master - LEARN_RATE * ratio_cols[None, :] * direction
    master_v_new = master_v - LEARN_RATE * ratio_entries * direction_v
    weights_mat, weights_vec = (
        lax.all_gather(master_new.astype(jnp.bfloat16), "dp", axis=0, tiled=True),
        lax.all_gather(master_v_new.astype(jnp.bfloat16), "dp", axis=0, tiled=True),
    )
    return (
        weights_mat.reshape(1, section_rows, columns),
        weights_vec,
        master_new.reshape(state_shape),
        first_new.reshape(state_shape),
        second_new.reshape(state_shape),
        master_v_new.reshape(vec_shape),
        first_v.reshape(vec_shape),
        second_v.reshape(vec_shape),
    )


def solution(mesh):
    in_specs = (
        P("dp", "tensor", "section", None),
        P("dp", None),
        P("tensor", "section", "dp", None, None),
        P("tensor", "section", "dp", None, None),
        P("tensor", "section", "dp", None, None),
        P("dp", None),
        P("dp", None),
        P("dp", None),
    )
    out_specs = (
        P("tensor", "section", None),
        P(),
        P("tensor", "section", "dp", None, None),
        P("tensor", "section", "dp", None, None),
        P("tensor", "section", "dp", None, None),
        P("dp", None),
        P("dp", None),
        P("dp", None),
    )
    return jax.shard_map(local, mesh=mesh, in_specs=in_specs, out_specs=out_specs, check_vma=False)
```

profile of v0, /device:TPU:0, one launch (start us, length us, event | category | flops | bytes accessed | tf_op | source)
XLA Modules:
  0.0 512.2 jit_solution(12687910160907905773)
XLA Ops:
  7.2 0.0 all-reduce.8.cloned.1.call-start
  7.2 9.8 %bitcast_convert_fusion = f32[800,4800]{1,0:T(8,128)} fusion(bf16[1,1,800,4800]{3,2,1,0:T(8,128)(2,1)} %param.12), kind=kLoop, calls=%fused_computation | loop fusion | flops 3840000 | bytes 23040000 | tf_op jit(solution)/shard_map/convert_element_type | solution.py:56
  17.0 170.8 %fusion = f32[64,4800]{1,0:T(8,128)S(1)} fusion(f32[800,4800]{1,0:T(8,128)} %bitcast_convert_fusion), kind=kCustom, calls=%all-reduce-scatter | all-reduce-scatter fusion | flops 4915201 | bytes 16589312
  187.9 3.8 collective-permute-start.2
  191.7 4.4 collective-permute-start.1
  196.1 2.3 collective-permute-start
  198.5 1.3 collective-permute-start.3
  199.8 0.9 convert_reduce_fusion
  200.7 0.0 all-reduce.8.cloned.1.call-update
  200.7 0.0 all-gather.3.cloned.1.call-start
  200.8 0.6 fusion.13
  202.0 77.2 %collective-permute-done.3 = f32[18,4800]{1,0:T(8,128)S(1)} collective-permute-done((f32[18,4800]{1,0:T(8,128)S(1)}, f32[18,4800]{1,0:T(8,128)S(1)}, u32[]{:S(2)}, u32[]{:S(2)}) %collective-permute-start.3) | collective-permute-done | bytes 345632
  279.2 22.9 %concatenate = f32[274,4800]{1,0:T(8,128)} concatenate(f32[18,4800]{1,0:T(8,128)S(1)} %collective-permute-done.3, f32[64,4800]{1,0:T(8,128)} %collective-permute-done.2, f32[64,4800]{1,0:T(8,128)} %collective-permute-done.1, f32[64,4800]{1,0:T(8,128)} %collective-permute-done, f32[64,4800]{1,0:T(8,128)S(1)} %fusion), dimensions={0} | concatenate | bytes 10521600
  302.2 3.9 multiply_reduce_fusion
  306.1 0.3 select_reduce_fusion.2
  306.4 66.5 %all-reduce.4 = (f32[4]{0:T(128)S(1)}, f32[4]{0:T(128)S(1)}) all-reduce(f32[4]{0:T(128)S(1)} %get-tuple-element.29, f32[4]{0:T(128)S(1)} %get-tuple-element.28), channel_id=1, replica_groups=mesh['dp'=16,'tensor'=4,'section'=2] {'dp','tensor','section'}, use_global_device_ids=true, to_apply=%region_6.0 | all-reduce | flops 8 | bytes 64 | tf_op jit(solution)/shard_map/psum | solution.py:70
  373.0 0.1 select_reduce_fusion
  373.2 2.5 fusion.4
  377.1 0.0 all-reduce.8.cloned.1.call-done
  377.2 0.8 fusion.9
  378.0 0.2 select_reduce_fusion.5
  378.2 38.7 %all-reduce.5 = (f32[8]{0:T(128)S(1)}, f32[8]{0:T(128)S(1)}) all-reduce(f32[8]{0:T(128)S(1)} %get-tuple-element.25, f32[8]{0:T(128)S(1)} %get-tuple-element.24), channel_id=1, replica_groups=mesh['dp'=16,'tensor'=4,'section'=2] {'dp'}, use_global_device_ids=true, to_apply=%region_12.0 | all-reduce | flops 16 | bytes 128 | tf_op jit(solution)/shard_map/psum | solution.py:71
  416.9 0.6 reshape.85
  417.5 0.6 reshape.86
  418.1 0.1 select_reduce_fusion.3
  418.3 0.6 reshape.84
  418.9 0.2 dynamic-update-slice
  419.1 71.6 %all-reduce = bf16[20800]{0:T(1024)(128)(2,1)} all-reduce(bf16[20800]{0:T(1024)(128)(2,1)S(1)} %dynamic-update-slice), channel_id=1, replica_groups=mesh['dp'=16,'tensor'=4,'section'=2] {'dp'}, use_global_device_ids=true, to_apply=%add | all-reduce | flops 20800 | bytes 83200
  490.7 1.9 copy.31
  492.7 1.9 copy.33
  494.6 1.9 copy.32
  496.6 8.8 %reshape.79 = bf16[1,800,4800]{2,1,0:T(8,128)(2,1)} reshape(bf16[16,50,4800]{2,1,0:T(8,128)(2,1)} %all-gather.3.cloned.1.call-done) | data formatting | bytes 15360000 | tf_op jit(solution)/shard_map/reshape | solution.py:83
  (34 shorter events, 0.2 us)
Async XLA Ops:
  7.2 370.0 %all-reduce.8.cloned.1.call-start = ((), (), s32[]{:S(2)}) async-start(), calls=%async_computation.1 | async-start | bytes 172032
  17.0 182.8 %copy-start.1 = (bf16[1,20800]{1,0:T(2,128)(2,1)S(1)}, bf16[1,20800]{1,0:T(2,128)(2,1)}, u32[]{:S(2)}) copy-start(bf16[1,20800]{1,0:T(2,128)(2,1)} %param.13) | copy-start | bytes 124804
  187.9 12.9 %copy-start.5 = (u32[128]{0:T(128)S(1)}, u32[128]{0:T(128)}, u32[]{:S(2)}) copy-start(u32[128]{0:T(128)} %constant.69) | copy-start | bytes 1540
  187.9 91.4 %collective-permute-start.2 = (f32[64,4800]{1,0:T(8,128)S(1)}, f32[64,4800]{1,0:T(8,128)}, u32[]{:S(2)}, u32[]{:S(2)}) collective-permute-start(f32[64,4800]{1,0:T(8,128)S(1)} %fusion), channel_id=1, source_target_pairs={{0,24},{8,32},{16,40},{24,48},{32,56},{40,64},{48,72},{56,80},{64,... | collective-permute-start | bytes 3686408
  191.7 87.6 %collective-permute-start.1 = (f32[64,4800]{1,0:T(8,128)S(1)}, f32[64,4800]{1,0:T(8,128)}, u32[]{:S(2)}, u32[]{:S(2)}) collective-permute-start(f32[64,4800]{1,0:T(8,128)S(1)} %fusion), channel_id=1, source_target_pairs={{0,16},{8,24},{16,32},{24,40},{32,48},{40,56},{48,64},{56,72},{64,... | collective-permute-start | bytes 3686408
  196.1 83.1 %collective-permute-start = (f32[64,4800]{1,0:T(8,128)S(1)}, f32[64,4800]{1,0:T(8,128)}, u32[]{:S(2)}, u32[]{:S(2)}) collective-permute-start(f32[64,4800]{1,0:T(8,128)S(1)} %fusion), channel_id=1, source_target_pairs={{0,8},{8,16},{16,24},{24,32},{32,40},{40,48},{48,56},{56,64},{64,7... | collective-permute-start | bytes 3686408
  198.5 80.8 %collective-permute-start.3 = (f32[18,4800]{1,0:T(8,128)S(1)}, f32[18,4800]{1,0:T(8,128)S(1)}, u32[]{:S(2)}, u32[]{:S(2)}) collective-permute-start(f32[18,4800]{1,0:T(8,128)S(1)} %slice), channel_id=1, source_target_pairs={{0,32},{8,40},{16,48},{24,56},{32,64},{40,72},{48,80},{56,88},{64,... | collective-permute-start | bytes 1036808
  200.7 295.9 %all-gather.3.cloned.1.call-start = ((), (), s32[]{:S(2)}) async-start(), calls=%async_computation | async-start | bytes 9261056 | tf_op jit(solution)/shard_map/all_gather | solution.py:79
  202.0 100.2 %copy-start = (f32[1,1,1,50,4800]{4,2,3,1,0:T(1,128)S(1)}, f32[1,1,1,50,4800]{4,2,3,1,0:T(1,128)}, u32[]{:S(2)}) copy-start(f32[1,1,1,50,4800]{4,2,3,1,0:T(1,128)} %param.14) | copy-start | bytes 2880004
  302.2 3.9 copy-start.6
  302.2 3.9 copy-start.7
  373.1 3.9 copy-start.4
  373.2 3.9 copy-start.2
  373.2 3.9 copy-start.3
  373.2 4.8 copy-start.8
  373.2 4.8 copy-start.9
Sparse Core Ops, SparseCore 0:
  200.8 141.9 all-reduce.7
  375.8 70.2 all-gather.2
where the time goes:
time: 513 us; the launch traced here: 512 us
  blocking collectives  348 us (68%)
  waiting for transfers between devices  77.3 us (15%)
  local copies, waits for them, and re-layouts  40.3 us (8%)
  other arithmetic  18.8 us (4%)
  between operations  16.2 us (3%)
  starting transfers between devices  12 us (2%)
    unnamed x2, blocking collectives  242 us
    unnamed x7, waiting for transfers between devices  77.3 us
    psum x1, blocking collectives, local(): lax.psum((weight_mat_sq, update_mat_sq), ('dp', 'tensor', 'section'))  66.5 us
    psum x1, blocking collectives, local(): wsum_vec, usum_vec = lax.psum((weight_vec_sq, update_vec_sq), 'dp')  38.7 us
    unnamed x28, local copies, waits for them, and re-layouts  29.7 us
    unnamed x5, starting transfers between devices  11.9 us
  transfers between devices with their start and end apart: 6, of which 1 were waited for; matrix products, arithmetic and copies ran while one was open for 8% of the time, Pallas kernels for 0%

commit v1 on v0

--- a/solution.py
+++ b/solution.py
@@ -31,14 +31,17 @@
 
 
 def local(grad_mat, grad_vec, master_mat, first_mat, second_mat, master_vec, first_vec, second_vec):
+    n_dp = lax.axis_size("dp")
     tensor_count = lax.axis_size("tensor")
     section_rows = grad_mat.shape[2]
     columns = grad_mat.shape[3]
     vec_length = grad_vec.shape[1]
     state_shape = master_mat.shape
     vec_shape = master_vec.shape
+    owned_rows = state_shape[3]
     owned_vec = vec_shape[1]
-    master = master_mat.reshape(-1, columns)
+    assert owned_vec <= columns and owned_rows * n_dp == section_rows
+    master = master_mat.reshape(owned_rows, columns)
     master_v = master_vec.reshape(owned_vec)
     bounds_mat = [
         0,
@@ -51,36 +54,47 @@
     bounds_vec = [0, D, 2 * D, 5 * D, 6 * D, 7 * D, 8 * D, 8 * D + FF, 9 * D + FF]
     vec_index = lax.axis_index("dp") * owned_vec + lax.iota(jnp.int32, owned_vec)
     masks_vec = segment_masks(vec_index, bounds_vec)
-    weight_mat_sq = jnp.sum(masks_mat * jnp.sum(master * master, axis=0)[None, :], axis=1)
-    weight_vec_sq = jnp.sum(masks_vec * (master_v * master_v)[None, :], axis=1)
-    local_grad = grad_mat.reshape(section_rows, columns).astype(jnp.float32)
-    local_vec = grad_vec.reshape(vec_length).astype(jnp.float32)
-    gradient, gradient_v = (
-        lax.psum_scatter(local_grad, "dp", scatter_dimension=0, tiled=True),
-        lax.psum_scatter(local_vec, "dp", scatter_dimension=0, tiled=True),
-    )
+
+    local_grad = grad_mat.reshape(n_dp, owned_rows, columns).astype(jnp.float32)
+    local_vec = grad_vec.reshape(n_dp, 1, owned_vec).astype(jnp.float32)
+    local_vec = jnp.pad(local_vec, ((0, 0), (0, 0), (0, columns - owned_vec)))
+    payload = jnp.concatenate([local_grad, local_vec], axis=1)
+    summed = lax.optimization_barrier(lax.psum_scatter(payload, "dp", scatter_dimension=0, tiled=True))
+    gradient = summed[0, :owned_rows]
+    gradient_v = summed[0, owned_rows, :owned_vec]
+
     first_new, second_new, direction = adam_direction(
-        gradient, master, first_mat.reshape(-1, columns), second_mat.reshape(-1, columns), DECAY_MAT
+        gradient, master, first_mat.reshape(owned_rows, columns), second_mat.reshape(owned_rows, columns), DECAY_MAT
     )
     first_v, second_v, direction_v = adam_direction(
         gradient_v, master_v, first_vec.reshape(owned_vec), second_vec.reshape(owned_vec), 0.0
     )
+    weight_mat_sq = jnp.sum(masks_mat * jnp.sum(master * master, axis=0)[None, :], axis=1)
+    weight_vec_sq = jnp.sum(masks_vec * (master_v * master_v)[None, :], axis=1)
     update_mat_sq = jnp.sum(masks_mat * jnp.sum(direction * direction, axis=0)[None, :], axis=1)
     update_vec_sq = jnp.sum(masks_vec * (direction_v * direction_v)[None, :], axis=1)
-    wsum_mat, usum_mat = lax.psum((weight_mat_sq, update_mat_sq), ("dp", "tensor", "section"))
-    wsum_vec, usum_vec = lax.psum((weight_vec_sq, update_vec_sq), "dp")
+
+    vec_owner = (lax.axis_index("tensor") == 0) & (lax.axis_index("section") == 0)
+    vec_part = jnp.where(vec_owner, jnp.concatenate([weight_vec_sq, update_vec_sq]), 0.0)
+    sums = lax.psum(jnp.concatenate([weight_mat_sq, update_mat_sq, vec_part]), ("dp", "tensor", "section"))
+    n_mat = weight_mat_sq.shape[0]
+    n_vec = weight_vec_sq.shape[0]
+    wsum_mat, usum_mat = sums[:n_mat], sums[n_mat : 2 * n_mat]
+    wsum_vec, usum_vec = sums[2 * n_mat : 2 * n_mat + n_vec], sums[2 * n_mat + n_vec :]
     ratio_mat = jnp.sqrt(wsum_mat) / jnp.sqrt(usum_mat)
     ratio_vec = jnp.sqrt(wsum_vec) / jnp.sqrt(usum_vec)
     ratio_cols = jnp.sum(masks_mat * ratio_mat[:, None], axis=0)
     ratio_entries = jnp.sum(masks_vec * ratio_vec[:, None], axis=0)
     master_new = master - LEARN_RATE * ratio_cols[None, :] * direction
     master_v_new = master_v - LEARN_RATE * ratio_entries * direction_v
-    weights_mat, weights_vec = (
-        lax.all_gather(master_new.astype(jnp.bfloat16), "dp", axis=0, tiled=True),
-        lax.all_gather(master_v_new.astype(jnp.bfloat16), "dp", axis=0, tiled=True),
-    )
+
+    weights_v_row = jnp.pad(master_v_new.astype(jnp.bfloat16), (0, columns - owned_vec))[None, :]
+    weights_rows = jnp.concatenate([master_new.astype(jnp.bfloat16), weights_v_row], axis=0)
+    gathered = lax.all_gather(weights_rows, "dp", axis=0, tiled=False)
+    weights_mat = gathered[:, :owned_rows].reshape(1, section_rows, columns)
+    weights_vec = gathered[:, owned_rows, :owned_vec].reshape(vec_length)
     return (
-        weights_mat.reshape(1, section_rows, columns),
+        weights_mat,
         weights_vec,
         master_new.reshape(state_shape),
         first_new.reshape(state_shape),

time: 513 us -> 303 us (0.59)
  blocking collectives: 348 us -> 64.3 us
  waiting for transfers between devices: 77.3 us -> 172 us
  local copies, waits for them, and re-layouts: 40.3 us -> 20.9 us
  starting transfers between devices: 12 us -> 0.08 us
  other arithmetic: 18.8 us -> 30.2 us
    unnamed x2 -> x0, blocking collectives: 242 us -> none
    all_gather x1, waiting for transfers between devices: 0.01 us -> 58.2 us  [local(): gathered = lax.all_gather(weights_rows, 'dp', axis=0, tiled=False)]
    psum x2 -> x1, blocking collectives: 105 us -> 64.3 us  [local(): lax.psum(jnp.concatenate([weight_mat_sq, update_mat_sq, vec_part]), ('dp'...]
    unnamed x7 -> x3, waiting for transfers between devices: 77.3 us -> 114 us
    unnamed x28 -> x26, local copies, waits for them, and re-layouts: 29.7 us -> 2.06 us
    unnamed x5 -> x1, starting transfers between devices: 11.9 us -> 0.04 us
    unnamed x0 -> x3, other arithmetic: none -> 11.2 us
    concatenate x0 -> x2, other arithmetic: none -> 10.8 us  [the longest x1 10.7 us: local(): payload = jnp.concatenate([local_grad, local_vec], axis=1)]
  transfers between devices with their start and end apart: 6 -> 2, of which waited for: 1 -> 2; matrix products, arithmetic and copies ran while one was open for 8% -> 4% of each run, Pallas kernels for 0% -> 0%
where the time goes in v1:
time: 303 us; the launch traced here: 302 us
  waiting for transfers between devices  172 us (57%)
  blocking collectives  64.3 us (21%)
  other arithmetic  30.2 us (10%)
  local copies, waits for them, and re-layouts  20.9 us (7%)
  between operations  14.2 us (5%)
    unnamed x3, waiting for transfers between devices  114 us
    psum x1, blocking collectives, local(): lax.psum(jnp.concatenate([weight_mat_sq, update_mat_sq, vec_part]), ('dp'...  64.3 us
    all_gather x1, waiting for transfers between devices, local(): gathered = lax.all_gather(weights_rows, 'dp', axis=0, tiled=False)  58.2 us
    unnamed x3, other arithmetic  11.2 us
    concatenate x1, other arithmetic, local(): payload = jnp.concatenate([local_grad, local_vec], axis=1)  10.7 us
    reshape x1, local copies, waits for them, and re-layouts, local(): weights_mat = gathered[:, :owned_rows].reshape(1, section_rows, columns)  8.78 us
    convert_element_type x1, local copies, waits for them, and re-layouts, local(): local_grad = grad_mat.reshape(n_dp, owned_rows, columns).astype(jnp.float32)  7.85 us
  transfers between devices with their start and end apart: 2, of which 2 were waited for; matrix products, arithmetic and copies ran while one was open for 4% of the time, Pallas kernels for 0%

profile of v1, /device:TPU:0, one launch (start us, length us, event | category | flops | bytes accessed | tf_op | source)
XLA Modules:
  0.0 301.9 jit_solution(7704911711402890190)
XLA Ops:
  7.2 0.0 reduce-scatter.4.cloned.1.call-start
  7.2 7.8 %convert_element_type.28 = bf16[16,50,4800]{2,1,0:T(8,128)(2,1)} reshape(bf16[1,1,800,4800]{3,2,1,0:T(8,128)(2,1)} %param.12) | data formatting | bytes 15360000 | tf_op jit(solution)/shard_map/convert_element_type | solution.py:58
  15.1 0.2 reduce
  15.3 0.1 convert_element_type.32
  15.4 10.7 %fusion.2 = f32[16,51,4800]{2,1,0:T(8,128)} fusion(bf16[16,1,1300]{2,1,0:T(2,128)(2,1)S(1)} %convert_element_type.32, bf16[16,50,4800]{2,1,0:T(8,128)(2,1)} %convert_element_type.28), kind=kLoop, calls=%fused_computation.3 | loop fusion | flops 23500800 | bytes 23388800 | tf_op jit(solution)/shard_map/concatenate | solution.py:61
  26.3 0.0 all-gather.4.cloned.1.call-start
  26.3 1.0 copy-done.3
  27.4 1.9 bitcast_multiply_fusion.3
  29.3 114.0 %reduce-scatter.4.cloned.1.call-done = f32[1,51,4800]{2,1,0:T(8,128)} async-done(((f32[16,51,4800]{2,1,0:T(8,128)}), f32[1,51,4800]{2,1,0:T(8,128)}) %reduce-scatter.4.cloned.1.call-update) | async-done | bytes 979216
  143.3 1.4 multiply_reduce_fusion.1
  144.8 0.2 select_reduce_fusion.5
  145.0 0.1 broadcast_select_fusion
  145.1 2.9 multiply_reduce_fusion
  148.0 0.3 select_reduce_fusion.2
  148.3 0.1 pad_maximum_fusion
  148.5 64.3 %psum.7 = f32[24]{0:T(128)S(1)} all-reduce(f32[24]{0:T(128)S(1)} %pad_maximum_fusion), channel_id=1, replica_groups=mesh['dp'=16,'tensor'=4,'section'=2] {'dp','tensor','section'}, use_global_device_ids=true, to_apply=%region_7.8 | all-reduce | flops 24 | bytes 192 | tf_op jit(solution)/shard_map/psum | solution.py:79
  212.8 0.1 rsqrt_multiply_fusion
  212.9 0.1 rsqrt_multiply_fusion.1
  212.9 0.1 select_reduce_fusion.3
  213.1 0.1 select_reduce_fusion
  213.3 0.1 fusion.11
  213.4 0.9 maximum_bitcast_fusion
  214.3 0.0 all-gather.4.cloned.1.call-update
  214.3 0.5 copy-done.2
  214.8 0.1 copy_multiply_fusion
  214.9 0.6 multiply_subtract_fusion
  215.5 0.5 copy-done.4
  216.0 10.1 %fusion.15 = (f32[1,1,1,50,4800]{4,2,3,1,0:T(1,128)}, f32[1,1,1,50,4800]{4,0,3,2,1:T(1,128)}, f32[1,1,1,50,4800]{4,2,3,1,0:T(1,128)}) fusion(f32[1,1,1,50,4800]{4,2,3,1,0:T(1,128)S(1)} %copy-done, f32[4800]{0:T(1024)S(1)} %broadcast_multiply_fusion, f32[1,50,4800]{2,1,0:T(8,128)S(1)} %bitcast.68, f32[1,1,1,50,4800]{4,2,3,1,0:T(1,128)S(1)} %copy-done.4, ...), kind=kLoop, calls=%fused_computation.28 | loop fusion | flops 3360000 | bytes 6739200
  226.1 58.2 %all-gather.4.cloned.1.call-done = bf16[16,51,4800]{2,1,0:T(8,128)(2,1)} async-done(((bf16[1,51,4800]{2,1,0:T(8,128)(2,1)}), bf16[16,51,4800]{2,1,0:T(8,128)(2,1)}) %all-gather.4.cloned.1.call-update) | async-done | bytes 7833616 | tf_op jit(solution)/shard_map/all_gather | solution.py:93
  284.3 8.8 %reshape.155 = bf16[1,800,4800]{2,1,0:T(8,128)(2,1)} reshape(bf16[16,50,4800]{2,1,0:T(8,128)(2,1)} %bitcast.67) | data formatting | bytes 15360000 | tf_op jit(solution)/shard_map/reshape | solution.py:94
  293.1 1.3 slice_reduce_fusion
  294.3 0.8 reshape_squeeze.3
  (30 shorter events, 0.2 us)
Async XLA Ops:
  7.2 7.9 %copy-start.5 = (bf16[1,20800]{1,0:T(2,128)(2,1)S(1)}, bf16[1,20800]{1,0:T(2,128)(2,1)}, u32[]{:S(2)}) copy-start(bf16[1,20800]{1,0:T(2,128)(2,1)} %param.13) | copy-start | bytes 124804
  7.2 136.2 %reduce-scatter.4.cloned.1.call-start = ((), (), s32[]{:S(2)}) async-start(), calls=%async_computation.2 | async-start | bytes 18522112
  26.2 1.2 copy-start.3
  26.2 117.1 %copy-start.6 = (f32[1,1300]{1,0:T(1,128)S(1)}, f32[1,1300]{1,0:T(1,128)}, u32[]{:S(2)}) copy-start(f32[1,1300]{1,0:T(1,128)} %param.17) | copy-start | bytes 15604
  26.2 117.1 %copy-start.7 = (f32[1,1300]{1,0:T(1,128)S(1)}, f32[1,1300]{1,0:T(1,128)}, u32[]{:S(2)}) copy-start(f32[1,1300]{1,0:T(1,128)} %param.18) | copy-start | bytes 15604
  26.2 117.1 %copy-start.8 = (f32[1,1300]{1,0:T(1,128)S(1)}, f32[1,1300]{1,0:T(1,128)}, u32[]{:S(2)}) copy-start(f32[1,1300]{1,0:T(1,128)} %param.19) | copy-start | bytes 15604
  26.2 118.5 %copy-start.11 = (s32[8]{0:T(128)S(1)}, s32[8]{0:T(128)}, u32[]{:S(2)}) copy-start(s32[8]{0:T(128)} %constant.70.clone) | copy-start | bytes 100
  26.2 118.5 %copy-start.12 = (s32[8]{0:T(128)S(1)}, s32[8]{0:T(128)}, u32[]{:S(2)}) copy-start(s32[8]{0:T(128)} %constant.71.clone) | copy-start | bytes 100
  26.3 118.8 %copy-start = (f32[1,1,1,50,4800]{4,2,3,1,0:T(1,128)S(1)}, f32[1,1,1,50,4800]{4,2,3,1,0:T(1,128)}, u32[]{:S(2)}) copy-start(f32[1,1,1,50,4800]{4,2,3,1,0:T(1,128)} %param.14) | copy-start | bytes 2880004
  26.3 258.0 %all-gather.4.cloned.1.call-start = ((), (), s32[]{:S(2)}) async-start(), calls=%async_computation.1 | async-start | bytes 9261056 | tf_op jit(solution)/shard_map/all_gather | solution.py:93
  145.1 2.9 copy-start.9
  145.1 2.9 copy-start.10
  145.1 3.3 %copy-start.1 = (f32[1,51,4800]{2,1,0:T(8,128)S(1)}, f32[1,51,4800]{2,1,0:T(8,128)}, u32[]{:S(2)}) copy-start(f32[1,51,4800]{2,1,0:T(8,128)} %reduce-scatter.4.cloned.1.call-done) | copy-start | bytes 2937604
  213.4 1.4 copy-start.2
  214.8 1.2 copy-start.4
Sparse Core Ops, SparseCore 0:
  26.3 116.9 reduce-scatter.3
  214.4 69.8 all-gather.3

commit v2 on v1

--- a/solution.py
+++ b/solution.py
@@ -28,6 +28,17 @@
     lower = jnp.array(bounds[:-1], dtype=jnp.int32)[:, None]
     upper = jnp.array(bounds[1:], dtype=jnp.int32)[:, None]
     return ((position[None, :] >= lower) & (position[None, :] < upper)).astype(jnp.float32)
+
+
+def butterfly_sum(x, axes):
+    for axis in axes:
+        size = lax.axis_size(axis)
+        assert size & (size - 1) == 0
+        step = 1
+        while step < size:
+            x = x + lax.ppermute(x, axis, [(i, i ^ step) for i in range(size)])
+            step *= 2
+    return x
 
 
 def local(grad_mat, grad_vec, master_mat, first_mat, second_mat, master_vec, first_vec, second_vec):
@@ -76,7 +87,7 @@
 
     vec_owner = (lax.axis_index("tensor") == 0) & (lax.axis_index("section") == 0)
     vec_part = jnp.where(vec_owner, jnp.concatenate([weight_vec_sq, update_vec_sq]), 0.0)
-    sums = lax.psum(jnp.concatenate([weight_mat_sq, update_mat_sq, vec_part]), ("dp", "tensor", "section"))
+    sums = butterfly_sum(jnp.concatenate([weight_mat_sq, update_mat_sq, vec_part]), ("section", "tensor", "dp"))
     n_mat = weight_mat_sq.shape[0]
     n_vec = weight_vec_sq.shape[0]
     wsum_mat, usum_mat = sums[:n_mat], sums[n_mat : 2 * n_mat]

time: 303 us -> 268 us (0.88)
  blocking collectives: 64.3 us -> 0 us
  waiting for transfers between devices: 172 us -> 189 us
  starting transfers between devices: 0.08 us -> 12.6 us
    psum x1 -> x0, blocking collectives: 64.3 us -> none  [local(): lax.psum(jnp.concatenate([weight_mat_sq, update_mat_sq, vec_part]), ('dp'...]
    ppermute x0 -> x7, waiting for transfers between devices: none -> 14.5 us  [butterfly_sum(): x = x + lax.ppermute(x, axis, [(i, i ^ step) for i in range(size)])]
    ppermute x0 -> x7, starting transfers between devices: none -> 12.5 us  [butterfly_sum(): x = x + lax.ppermute(x, axis, [(i, i ^ step) for i in range(size)])]
  transfers between devices with their start and end apart: 2 -> 9, of which waited for: 2 -> 9; matrix products, arithmetic and copies ran while one was open for 4% -> 5% of each run, Pallas kernels for 0% -> 0%
where the time goes in v2:
time: 268 us; the launch traced here: 267 us
  waiting for transfers between devices  189 us (71%)
  other arithmetic  30 us (11%)
  local copies, waits for them, and re-layouts  20.4 us (8%)
  between operations  14.3 us (5%)
  starting transfers between devices  12.6 us (5%)
    unnamed x3, waiting for transfers between devices  114 us
    all_gather x1, waiting for transfers between devices, local(): gathered = lax.all_gather(weights_rows, 'dp', axis=0, tiled=False)  60.8 us
    ppermute x7, waiting for transfers between devices, butterfly_sum(): x = x + lax.ppermute(x, axis, [(i, i ^ step) for i in range(size)])  14.5 us
    ppermute x7, starting transfers between devices, butterfly_sum(): x = x + lax.ppermute(x, axis, [(i, i ^ step) for i in range(size)])  12.5 us
    unnamed x3, other arithmetic  11.2 us
    concatenate x1, other arithmetic, local(): payload = jnp.concatenate([local_grad, local_vec], axis=1)  10.7 us
    reshape x1, local copies, waits for them, and re-layouts, local(): weights_mat = gathered[:, :owned_rows].reshape(1, section_rows, columns)  8.78 us
    convert_element_type x1, local copies, waits for them, and re-layouts, local(): local_grad = grad_mat.reshape(n_dp, owned_rows, columns).astype(jnp.float32)  7.85 us
  transfers between devices with their start and end apart: 9, of which 9 were waited for; matrix products, arithmetic and copies ran while one was open for 5% of the time, Pallas kernels for 0%

profile of v2, /device:TPU:0, one launch (start us, length us, event | category | flops | bytes accessed | tf_op | source)
XLA Modules:
  0.0 266.6 jit_solution(13134282096747706945)
XLA Ops:
  7.2 7.8 %convert_element_type.28 = bf16[16,50,4800]{2,1,0:T(8,128)(2,1)} reshape(bf16[1,1,800,4800]{3,2,1,0:T(8,128)(2,1)} %param.12) | data formatting | bytes 15360000 | tf_op jit(solution)/shard_map/convert_element_type | solution.py:69
  15.1 0.2 reduce
  15.4 10.7 %fusion.2 = f32[16,51,4800]{2,1,0:T(8,128)} fusion(bf16[16,1,1300]{2,1,0:T(2,128)(2,1)S(1)} %convert_element_type.32, bf16[16,50,4800]{2,1,0:T(8,128)(2,1)} %convert_element_type.28), kind=kLoop, calls=%fused_computation.3 | loop fusion | flops 23500800 | bytes 23388800 | tf_op jit(solution)/shard_map/concatenate | solution.py:72
  26.4 1.0 copy-done.3
  27.4 1.9 bitcast_multiply_fusion.3
  29.3 114.0 %reduce-scatter.4.cloned.1.call-done = f32[1,51,4800]{2,1,0:T(8,128)} async-done(((f32[16,51,4800]{2,1,0:T(8,128)}), f32[1,51,4800]{2,1,0:T(8,128)}) %reduce-scatter.4.cloned.1.call-update) | async-done | bytes 979216
  143.3 1.4 multiply_reduce_fusion.1
  144.8 0.2 select_reduce_fusion.5
  145.1 2.6 multiply_reduce_fusion
  147.8 0.3 select_reduce_fusion.2
  148.2 1.1 collective-permute-done
  149.4 1.5 collective-permute-start.1
  150.9 2.1 collective-permute-done.1
  153.0 3.0 %collective-permute-start.2 = (f32[24]{0:T(128)S(1)}, f32[24]{0:T(128)S(1)}, u32[]{:S(2)}, u32[]{:S(2)}) collective-permute-start(f32[24]{0:T(128)S(1)} %add.116), channel_id=1, source_target_pairs={{0,4},{2,6},{4,0},{6,2},{1,5},{3,7},{5,1},{7,3},{8,12},{10,14},{12... | collective-permute-start | bytes 296 | tf_op jit(solution)/shard_map/ppermute | solution.py:39
  156.0 2.0 collective-permute-done.2
  158.1 1.3 collective-permute-start.3
  159.4 2.3 collective-permute-done.3
  161.6 2.8 %collective-permute-start.4 = (f32[24]{0:T(128)S(1)}, f32[24]{0:T(128)S(1)}, u32[]{:S(2)}, u32[]{:S(2)}) collective-permute-start(f32[24]{0:T(128)S(1)} %add.118), channel_id=1, source_target_pairs={{0,16},{8,24},{16,0},{24,8},{32,48},{40,56},{48,32},{56,40},{64,80... | collective-permute-start | bytes 296 | tf_op jit(solution)/shard_map/ppermute | solution.py:39
  164.5 2.2 collective-permute-done.4
  166.7 1.1 collective-permute-start.5
  167.9 2.4 collective-permute-done.5
  170.3 2.7 %collective-permute-start.6 = (f32[24]{0:T(128)S(1)}, f32[24]{0:T(128)S(1)}, u32[]{:S(2)}, u32[]{:S(2)}) collective-permute-start(f32[24]{0:T(128)S(1)} %add.120), channel_id=1, source_target_pairs={{0,64},{8,72},{16,80},{24,88},{32,96},{40,104},{48,112},{56,120},{... | collective-permute-start | bytes 296 | tf_op jit(solution)/shard_map/ppermute | solution.py:39
  173.1 2.3 collective-permute-done.6
  175.6 0.1 select_reduce_fusion
  176.0 0.9 maximum_bitcast_fusion
  177.0 0.6 multiply_subtract_fusion
  177.6 0.4 copy-done.4
  178.1 10.1 %fusion.15 = (f32[1,1,1,50,4800]{4,2,3,1,0:T(1,128)}, f32[1,1,1,50,4800]{4,0,3,2,1:T(1,128)}, f32[1,1,1,50,4800]{4,2,3,1,0:T(1,128)}) fusion(f32[1,1,1,50,4800]{4,2,3,1,0:T(1,128)S(1)} %copy-done, f32[4800]{0:T(1024)S(1)} %broadcast_multiply_fusion, f32[1,50,4800]{2,1,0:T(8,128)S(1)} %bitcast.68, f32[1,1,1,50,4800]{4,2,3,1,0:T(1,128)S(1)} %copy-done.4, ...), kind=kLoop, calls=%fused_computation.28 | loop fusion | flops 3360000 | bytes 6739200
  188.2 60.8 %all-gather.4.cloned.1.call-done = bf16[16,51,4800]{2,1,0:T(8,128)(2,1)} async-done(((bf16[1,51,4800]{2,1,0:T(8,128)(2,1)}), bf16[16,51,4800]{2,1,0:T(8,128)(2,1)}) %all-gather.4.cloned.1.call-update) | async-done | bytes 7833616 | tf_op jit(solution)/shard_map/all_gather | solution.py:104
  248.9 8.8 %reshape.155 = bf16[1,800,4800]{2,1,0:T(8,128)(2,1)} reshape(bf16[16,50,4800]{2,1,0:T(8,128)(2,1)} %bitcast.67) | data formatting | bytes 15360000 | tf_op jit(solution)/shard_map/reshape | solution.py:105
  257.7 1.3 slice_reduce_fusion
  259.0 0.8 reshape_squeeze.3
  (50 shorter events, 1.2 us)
Async XLA Ops:
  7.2 7.9 %copy-start.5 = (bf16[1,20800]{1,0:T(2,128)(2,1)S(1)}, bf16[1,20800]{1,0:T(2,128)(2,1)}, u32[]{:S(2)}) copy-start(bf16[1,20800]{1,0:T(2,128)(2,1)} %param.13) | copy-start | bytes 124804
  7.2 136.2 %reduce-scatter.4.cloned.1.call-start = ((), (), s32[]{:S(2)}) async-start(), calls=%async_computation.2 | async-start | bytes 18522112
  26.2 1.2 copy-start.3
  26.2 117.1 %copy-start.6 = (f32[1,1300]{1,0:T(1,128)S(1)}, f32[1,1300]{1,0:T(1,128)}, u32[]{:S(2)}) copy-start(f32[1,1300]{1,0:T(1,128)} %param.17) | copy-start | bytes 15604
  26.2 117.1 %copy-start.7 = (f32[1,1300]{1,0:T(1,128)S(1)}, f32[1,1300]{1,0:T(1,128)}, u32[]{:S(2)}) copy-start(f32[1,1300]{1,0:T(1,128)} %param.18) | copy-start | bytes 15604
  26.2 117.1 %copy-start.8 = (f32[1,1300]{1,0:T(1,128)S(1)}, f32[1,1300]{1,0:T(1,128)}, u32[]{:S(2)}) copy-start(f32[1,1300]{1,0:T(1,128)} %param.19) | copy-start | bytes 15604
  26.2 118.5 %copy-start.11 = (s32[8]{0:T(128)S(1)}, s32[8]{0:T(128)}, u32[]{:S(2)}) copy-start(s32[8]{0:T(128)} %constant.70.clone) | copy-start | bytes 100
  26.2 118.5 %copy-start.12 = (s32[8]{0:T(128)S(1)}, s32[8]{0:T(128)}, u32[]{:S(2)}) copy-start(s32[8]{0:T(128)} %constant.71.clone) | copy-start | bytes 100
  26.3 118.8 %copy-start = (f32[1,1,1,50,4800]{4,2,3,1,0:T(1,128)S(1)}, f32[1,1,1,50,4800]{4,2,3,1,0:T(1,128)}, u32[]{:S(2)}) copy-start(f32[1,1,1,50,4800]{4,2,3,1,0:T(1,128)} %param.14) | copy-start | bytes 2880004
  26.3 118.8 %copy-start.2 = (f32[1,1,1,50,4800]{4,2,3,1,0:T(1,128)S(1)}, f32[1,1,1,50,4800]{4,2,3,1,0:T(1,128)}, u32[]{:S(2)}) copy-start(f32[1,1,1,50,4800]{4,2,3,1,0:T(1,128)} %param.16) | copy-start | bytes 2880004
  26.3 222.6 %all-gather.4.cloned.1.call-start = ((), (), s32[]{:S(2)}) async-start(), calls=%async_computation.1 | async-start | bytes 9261056 | tf_op jit(solution)/shard_map/all_gather | solution.py:104
  145.1 2.7 copy-start.9
  145.1 2.7 copy-start.10
  145.1 27.9 %copy-start.1 = (f32[1,51,4800]{2,1,0:T(8,128)S(1)}, f32[1,51,4800]{2,1,0:T(8,128)}, u32[]{:S(2)}) copy-start(f32[1,51,4800]{2,1,0:T(8,128)} %reduce-scatter.4.cloned.1.call-done) | copy-start | bytes 2937604
  148.1 1.2 collective-permute-start
  149.4 3.6 %collective-permute-start.1 = (f32[24]{0:T(128)S(1)}, f32[24]{0:T(128)S(1)}, u32[]{:S(2)}, u32[]{:S(2)}) collective-permute-start(f32[24]{0:T(128)S(1)} %fusion.33), channel_id=1, source_target_pairs={{0,2},{2,0},{4,6},{6,4},{1,3},{3,1},{5,7},{7,5},{8,10},{10,8},{12,... | collective-permute-start | bytes 296 | tf_op jit(solution)/shard_map/ppermute | solution.py:39
  153.0 5.1 %collective-permute-start.2 = (f32[24]{0:T(128)S(1)}, f32[24]{0:T(128)S(1)}, u32[]{:S(2)}, u32[]{:S(2)}) collective-permute-start(f32[24]{0:T(128)S(1)} %add.116), channel_id=1, source_target_pairs={{0,4},{2,6},{4,0},{6,2},{1,5},{3,7},{5,1},{7,3},{8,12},{10,14},{12... | collective-permute-start | bytes 296 | tf_op jit(solution)/shard_map/ppermute | solution.py:39
  158.1 3.6 %collective-permute-start.3 = (f32[24]{0:T(128)S(1)}, f32[24]{0:T(128)S(1)}, u32[]{:S(2)}, u32[]{:S(2)}) collective-permute-start(f32[24]{0:T(128)S(1)} %add.117), channel_id=1, source_target_pairs={{0,8},{8,0},{16,24},{24,16},{32,40},{40,32},{48,56},{56,48},{64,72... | collective-permute-start | bytes 296 | tf_op jit(solution)/shard_map/ppermute | solution.py:39
  161.6 5.1 %collective-permute-start.4 = (f32[24]{0:T(128)S(1)}, f32[24]{0:T(128)S(1)}, u32[]{:S(2)}, u32[]{:S(2)}) collective-permute-start(f32[24]{0:T(128)S(1)} %add.118), channel_id=1, source_target_pairs={{0,16},{8,24},{16,0},{24,8},{32,48},{40,56},{48,32},{56,40},{64,80... | collective-permute-start | bytes 296 | tf_op jit(solution)/shard_map/ppermute | solution.py:39
  166.7 3.6 %collective-permute-start.5 = (f32[24]{0:T(128)S(1)}, f32[24]{0:T(128)S(1)}, u32[]{:S(2)}, u32[]{:S(2)}) collective-permute-start(f32[24]{0:T(128)S(1)} %add.119), channel_id=1, source_target_pairs={{0,32},{8,40},{16,48},{24,56},{32,0},{40,8},{48,16},{56,24},{64,96... | collective-permute-start | bytes 296 | tf_op jit(solution)/shard_map/ppermute | solution.py:39
  170.3 5.1 %collective-permute-start.6 = (f32[24]{0:T(128)S(1)}, f32[24]{0:T(128)S(1)}, u32[]{:S(2)}, u32[]{:S(2)}) collective-permute-start(f32[24]{0:T(128)S(1)} %add.120), channel_id=1, source_target_pairs={{0,64},{8,72},{16,80},{24,88},{32,96},{40,104},{48,112},{56,120},{... | collective-permute-start | bytes 296 | tf_op jit(solution)/shard_map/ppermute | solution.py:39
  176.9 1.2 copy-start.4
Sparse Core Ops, SparseCore 0:
  26.3 116.9 reduce-scatter.3
  177.0 71.9 all-gather.3

commit v3 on v2

--- a/solution.py
+++ b/solution.py
@@ -66,44 +66,62 @@
     vec_index = lax.axis_index("dp") * owned_vec + lax.iota(jnp.int32, owned_vec)
     masks_vec = segment_masks(vec_index, bounds_vec)
 
-    local_grad = grad_mat.reshape(n_dp, owned_rows, columns).astype(jnp.float32)
+    split = bounds_mat[3]
+    assert owned_vec <= split
+    grad_rows = grad_mat.reshape(n_dp, owned_rows, columns)
     local_vec = grad_vec.reshape(n_dp, 1, owned_vec).astype(jnp.float32)
-    local_vec = jnp.pad(local_vec, ((0, 0), (0, 0), (0, columns - owned_vec)))
-    payload = jnp.concatenate([local_grad, local_vec], axis=1)
-    summed = lax.optimization_barrier(lax.psum_scatter(payload, "dp", scatter_dimension=0, tiled=True))
-    gradient = summed[0, :owned_rows]
-    gradient_v = summed[0, owned_rows, :owned_vec]
+    local_vec = jnp.pad(local_vec, ((0, 0), (0, 0), (0, split - owned_vec)))
+    payload_a = jnp.concatenate([grad_rows[:, :, :split].astype(jnp.float32), local_vec], axis=1)
+    payload_b = grad_rows[:, :, split:].astype(jnp.float32)
+    summed_a = lax.optimization_barrier(lax.psum_scatter(payload_a, "dp", scatter_dimension=0, tiled=True))
+    summed_b = lax.optimization_barrier(lax.psum_scatter(payload_b, "dp", scatter_dimension=0, tiled=True))
+    vec_owner = (lax.axis_index("tensor") == 0) & (lax.axis_index("section") == 0)
 
-    first_new, second_new, direction = adam_direction(
-        gradient, master, first_mat.reshape(owned_rows, columns), second_mat.reshape(owned_rows, columns), DECAY_MAT
-    )
+    def matrix_chunk(gradient, lo, hi, extra):
+        chunk_master = master[:, lo:hi]
+        first_new, second_new, direction = adam_direction(
+            gradient,
+            chunk_master,
+            first_mat.reshape(owned_rows, columns)[:, lo:hi],
+            second_mat.reshape(owned_rows, columns)[:, lo:hi],
+            DECAY_MAT,
+        )
+        inside = [k for k in range(len(bounds_mat) - 1) if lo <= bounds_mat[k] and bounds_mat[k + 1] <= hi]
+        masks = masks_mat[inside[0] : inside[-1] + 1, lo:hi]
+        weight_sq = jnp.sum(masks * jnp.sum(chunk_master * chunk_master, axis=0)[None, :], axis=1)
+        update_sq = jnp.sum(masks * jnp.sum(direction * direction, axis=0)[None, :], axis=1)
+        n_mat = weight_sq.shape[0]
+        sums = butterfly_sum(jnp.concatenate([weight_sq, update_sq, extra]), ("section", "tensor", "dp"))
+        ratio = jnp.sqrt(sums[:n_mat]) / jnp.sqrt(sums[n_mat : 2 * n_mat])
+        ratio_cols = jnp.sum(masks * ratio[:, None], axis=0)
+        master_new = chunk_master - LEARN_RATE * ratio_cols[None, :] * direction
+        return master_new, first_new, second_new, sums[2 * n_mat :]
+
+    gradient_v = summed_a[0, owned_rows, :owned_vec]
     first_v, second_v, direction_v = adam_direction(
         gradient_v, master_v, first_vec.reshape(owned_vec), second_vec.reshape(owned_vec), 0.0
     )
-    weight_mat_sq = jnp.sum(masks_mat * jnp.sum(master * master, axis=0)[None, :], axis=1)
     weight_vec_sq = jnp.sum(masks_vec * (master_v * master_v)[None, :], axis=1)
-    update_mat_sq = jnp.sum(masks_mat * jnp.sum(direction * direction, axis=0)[None, :], axis=1)
     update_vec_sq = jnp.sum(masks_vec * (direction_v * direction_v)[None, :], axis=1)
-
-    vec_owner = (lax.axis_index("tensor") == 0) & (lax.axis_index("section") == 0)
     vec_part = jnp.where(vec_owner, jnp.concatenate([weight_vec_sq, update_vec_sq]), 0.0)
-    sums = butterfly_sum(jnp.concatenate([weight_mat_sq, update_mat_sq, vec_part]), ("section", "tensor", "dp"))
-    n_mat = weight_mat_sq.shape[0]
+    master_a, first_a, second_a, vec_sums = matrix_chunk(summed_a[0, :owned_rows], 0, split, vec_part)
     n_vec = weight_vec_sq.shape[0]
-    wsum_mat, usum_mat = sums[:n_mat], sums[n_mat : 2 * n_mat]
-    wsum_vec, usum_vec = sums[2 * n_mat : 2 * n_mat + n_vec], sums[2 * n_mat + n_vec :]
-    ratio_mat = jnp.sqrt(wsum_mat) / jnp.sqrt(usum_mat)
-    ratio_vec = jnp.sqrt(wsum_vec) / jnp.sqrt(usum_vec)
-    ratio_cols = jnp.sum(masks_mat * ratio_mat[:, None], axis=0)
+    ratio_vec = jnp.sqrt(vec_sums[:n_vec]) / jnp.sqrt(vec_sums[n_vec:])
     ratio_entries = jnp.sum(masks_vec * ratio_vec[:, None], axis=0)
-    master_new = master - LEARN_RATE * ratio_cols[None, :] * direction
     master_v_new = master_v - LEARN_RATE * ratio_entries * direction_v
 
-    weights_v_row = jnp.pad(master_v_new.astype(jnp.bfloat16), (0, columns - owned_vec))[None, :]
-    weights_rows = jnp.concatenate([master_new.astype(jnp.bfloat16), weights_v_row], axis=0)
-    gathered = lax.all_gather(weights_rows, "dp", axis=0, tiled=False)
-    weights_mat = gathered[:, :owned_rows].reshape(1, section_rows, columns)
-    weights_vec = gathered[:, owned_rows, :owned_vec].reshape(vec_length)
+    weights_v_row = jnp.pad(master_v_new.astype(jnp.bfloat16), (0, split - owned_vec))[None, :]
+    gathered_a = lax.all_gather(
+        jnp.concatenate([master_a.astype(jnp.bfloat16), weights_v_row], axis=0), "dp", axis=0, tiled=False
+    )
+    master_b, first_b, second_b, _ = matrix_chunk(summed_b[0], split, columns, jnp.zeros((0,), jnp.float32))
+    gathered_b = lax.all_gather(master_b.astype(jnp.bfloat16), "dp", axis=0, tiled=False)
+
+    weights_mat = jnp.concatenate([gathered_a[:, :owned_rows], gathered_b], axis=2).reshape(1, section_rows, columns)
+    weights_vec = gathered_a[:, owned_rows, :owned_vec].reshape(vec_length)
+    master_new = jnp.concatenate([master_a, master_b], axis=1)
+    first_new = jnp.concatenate([first_a, first_b], axis=1)
+    second_new = jnp.concatenate([second_a, second_b], axis=1)
     return (
         weights_mat,
         weights_vec,

time: 268 us -> 352 us (1.31)
  waiting for transfers between devices: 189 us -> 245 us
  starting transfers between devices: 12.6 us -> 24.5 us
  local copies, waits for them, and re-layouts: 20.4 us -> 31.1 us
  other arithmetic: 30 us -> 35.5 us
    unnamed x3 -> x6, waiting for transfers between devices: 114 us -> 153 us
    ppermute x7 -> x14, waiting for transfers between devices: 14.5 us -> 29.1 us  [butterfly_sum(): x = x + lax.ppermute(x, axis, [(i, i ^ step) for i in range(size)])]
    ppermute x7 -> x14, starting transfers between devices: 12.5 us -> 24.4 us  [butterfly_sum(): x = x + lax.ppermute(x, axis, [(i, i ^ step) for i in range(size)])]
    unnamed x3, other arithmetic: 11.2 us -> 2.62 us
    convert_element_type x1 -> x0, local copies, waits for them, and re-layouts: 7.85 us -> none  [local(): local_grad = grad_mat.reshape(n_dp, owned_rows, columns).astype(jnp.float32)]
    reshape x1 -> x2, local copies, waits for them, and re-layouts: 8.78 us -> 16.6 us  [the longest x1 8.78 us: local(): jnp.concatenate([gathered_a[:, :owned_rows], gathered_b], axis=2)]
    unnamed x26, local copies, waits for them, and re-layouts: 1.53 us -> 8.27 us
    convert_element_type x1 -> x3, other arithmetic: 0.13 us -> 5.97 us  [the longest x1 4.9 us: local(): payload_b = grad_rows[:, :, split:].astype(jnp.float32)]
  transfers between devices with their start and end apart: 9 -> 18, of which waited for: 9 -> 18; matrix products, arithmetic and copies ran while one was open for 5% -> 9% of each run, Pallas kernels for 0% -> 0%
where the time goes in v3:
time: 352 us; the launch traced here: 351 us
  waiting for transfers between devices  245 us (70%)
  other arithmetic  35.5 us (10%)
  local copies, waits for them, and re-layouts  31.1 us (9%)
  starting transfers between devices  24.5 us (7%)
  between operations  15.4 us (4%)
    unnamed x6, waiting for transfers between devices  153 us
    all_gather x1, waiting for transfers between devices, local(): lax.all_gather(master_b.astype(jnp.bfloat16), 'dp', axis=0, tiled=False)  46.9 us
    ppermute x14, waiting for transfers between devices, butterfly_sum(): x = x + lax.ppermute(x, axis, [(i, i ^ step) for i in range(size)])  29.1 us
    ppermute x14, starting transfers between devices, butterfly_sum(): x = x + lax.ppermute(x, axis, [(i, i ^ step) for i in range(size)])  24.4 us
    all_gather x1, waiting for transfers between devices, local(): lax.all_gather(jnp.concatenate([master_a.astype(jnp.bfloat16), weights_v_...  15.2 us
    reshape x1, local copies, waits for them, and re-layouts, local(): jnp.concatenate([gathered_a[:, :owned_rows], gathered_b], axis=2)  8.78 us
    unnamed x26, local copies, waits for them, and re-layouts  8.27 us
    reshape x1, local copies, waits for them, and re-layouts, local(): grad_rows = grad_mat.reshape(n_dp, owned_rows, columns)  7.81 us
  transfers between devices with their start and end apart: 18, of which 18 were waited for; matrix products, arithmetic and copies ran while one was open for 9% of the time, Pallas kernels for 0%

profile of v3, /device:TPU:0, one launch (start us, length us, event | category | flops | bytes accessed | tf_op | source)
XLA Modules:
  0.0 351.1 jit_solution(7431782052007080974)
XLA Ops:
  8.5 7.8 %reshape.136 = bf16[16,50,4800]{2,1,0:T(8,128)(2,1)} reshape(bf16[1,1,800,4800]{3,2,1,0:T(8,128)(2,1)} %param.12) | data formatting | bytes 15360000 | tf_op jit(solution)/shard_map/reshape | solution.py:71
  16.3 2.6 slice-done
  18.9 5.1 %fusion.2 = f32[16,51,3200]{2,1,0:T(8,128)} fusion(bf16[16,1,1300]{2,1,0:T(2,128)(2,1)S(1)} %convert_element_type.39, bf16[16,50,3200]{2,1,0:T(8,128)(2,1)S(1)} %slice-done), kind=kLoop, calls=%fused_computation.4 | loop fusion | flops 15667200 | bytes 15606400 | tf_op jit(solution)/shard_map/concatenate | solution.py:74
  24.1 4.9 %slice_convert_fusion = f32[16,50,1600]{2,1,0:T(8,128)} fusion(bf16[16,50,4800]{2,1,0:T(8,128)(2,1)} %reshape.136), kind=kLoop, calls=%fused_computation.5 | loop fusion | flops 1280000 | bytes 7680000 | tf_op jit(solution)/shard_map/convert_element_type | solution.py:75
  31.7 97.9 %reduce-scatter.7.cloned.1.call-done = f32[1,51,3200]{2,1,0:T(8,128)} async-done(((f32[16,51,3200]{2,1,0:T(8,128)}), f32[1,51,3200]{2,1,0:T(8,128)}) %reduce-scatter.7.cloned.1.call-update) | async-done | bytes 652816
  131.4 2.8 multiply_reduce_fusion
  137.2 2.1 collective-permute-done.1
  139.3 3.0 collective-permute-start.2
  142.3 2.1 collective-permute-done.2
  145.8 2.2 collective-permute-done.3
  148.0 2.5 collective-permute-start.4
  150.5 2.6 collective-permute-done.4
  154.4 2.2 collective-permute-done.5
  156.6 2.4 collective-permute-start.6
  164.0 55.4 %reduce-scatter.9.cloned.1.call-done = f32[1,50,1600]{2,1,0:T(8,128)} async-done(((f32[16,50,1600]{2,1,0:T(8,128)}), f32[1,50,1600]{2,1,0:T(8,128)}) %reduce-scatter.9.cloned.1.call-update) | async-done | bytes 320016
  219.4 2.1 multiply_reduce_fusion.2
  227.6 2.1 collective-permute-done.8
  231.0 3.0 collective-permute-start.9
  234.1 2.0 collective-permute-done.9
  237.3 2.4 collective-permute-done.10
  239.7 2.6 collective-permute-start.11
  242.4 2.4 collective-permute-done.11
  246.0 2.4 collective-permute-done.12
  248.4 2.6 collective-permute-start.13
  250.9 2.5 collective-permute-done.13
  257.9 1.9 copy.30
  259.8 1.9 copy.31
  261.9 1.9 copy.29
  264.4 15.2 %all-gather.7.cloned.1.call-done = bf16[16,51,3200]{2,1,0:T(8,128)(2,1)} async-done(((bf16[1,51,3200]{2,1,0:T(8,128)(2,1)}), bf16[16,51,3200]{2,1,0:T(8,128)(2,1)}) %all-gather.7.cloned.1.call-update) | async-done | bytes 5222416 | tf_op jit(solution)/shard_map/all_gather | solution.py:114
  281.6 46.9 %all-gather.9.cloned.1.call-done = bf16[16,50,1600]{2,1,0:T(8,128)(2,1)} async-done(((bf16[1,50,1600]{2,1,0:T(8,128)(2,1)}), bf16[16,50,1600]{2,1,0:T(8,128)(2,1)}) %all-gather.9.cloned.1.call-update) | async-done | bytes 2560016 | tf_op jit(solution)/shard_map/all_gather | solution.py:118
  328.5 7.2 %pad_maximum_fusion = bf16[16,50,4800]{2,1,0:T(8,128)(2,1)} fusion(bf16[16,50,1600]{2,1,0:T(8,128)(2,1)} %all-gather.9.cloned.1.call-done, bf16[16,50,3200]{2,1,0:T(8,128)(2,1)} %bitcast.52), kind=kLoop, calls=%fused_computation.2 | loop fusion | flops 15360000 | bytes 15360000 | tf_op jit(solution)/shard_map/concatenate | solution.py:120
  335.7 8.8 %reshape.139 = bf16[1,800,4800]{2,1,0:T(8,128)(2,1)} reshape(bf16[16,50,4800]{2,1,0:T(8,128)(2,1)} %pad_maximum_fusion) | data formatting | bytes 15360000 | tf_op jit(solution)/shard_map/reshape | solution.py:120
  (87 shorter events, 31.8 us)
Async XLA Ops:
  7.2 122.5 %reduce-scatter.7.cloned.1.call-start = ((), (), s32[]{:S(2)}) async-start(), calls=%async_computation.4 | async-start | bytes 12185600
  16.3 2.6 slice-start
  24.1 5.1 %copy-start.1 = (f32[1,1,1,50,4800]{4,2,3,1,0:T(1,128)S(1)}, f32[1,1,1,50,4800]{4,2,3,1,0:T(1,128)}, u32[]{:S(2)}) copy-start(f32[1,1,1,50,4800]{4,2,3,1,0:T(1,128)} %param.14) | copy-start | bytes 2880004
  24.1 195.3 %reduce-scatter.9.cloned.1.call-start = ((), (), s32[]{:S(2)}) async-start(), calls=%async_computation.5 | async-start | bytes 6336512
  29.0 1.2 copy-start.2
  29.0 2.6 copy-start.8
  29.0 2.6 copy-start.9
  29.0 100.6 %copy-start.3 = (f32[1,1300]{1,0:T(1,128)S(1)}, f32[1,1300]{1,0:T(1,128)}, u32[]{:S(2)}) copy-start(f32[1,1300]{1,0:T(1,128)} %param.17) | copy-start | bytes 15604
  29.0 100.6 %copy-start.4 = (f32[1,1300]{1,0:T(1,128)S(1)}, f32[1,1300]{1,0:T(1,128)}, u32[]{:S(2)}) copy-start(f32[1,1300]{1,0:T(1,128)} %param.18) | copy-start | bytes 15604
  29.0 100.6 %copy-start.5 = (f32[1,1300]{1,0:T(1,128)S(1)}, f32[1,1300]{1,0:T(1,128)}, u32[]{:S(2)}) copy-start(f32[1,1300]{1,0:T(1,128)} %param.19) | copy-start | bytes 15604
  29.1 102.0 %copy-start.6 = (s32[8]{0:T(128)S(1)}, s32[8]{0:T(128)}, u32[]{:S(2)}) copy-start(s32[8]{0:T(128)} %constant.79.clone) | copy-start | bytes 100
  29.1 102.0 %copy-start.7 = (s32[8]{0:T(128)S(1)}, s32[8]{0:T(128)}, u32[]{:S(2)}) copy-start(s32[8]{0:T(128)} %constant.78.clone) | copy-start | bytes 100
  29.1 250.4 %all-gather.7.cloned.1.call-start = ((), (), s32[]{:S(2)}) async-start(), calls=%async_computation.2 | async-start | bytes 6092800 | tf_op jit(solution)/shard_map/all_gather | solution.py:114
  134.5 1.2 collective-permute-start
  135.7 3.6 %collective-permute-start.1 = (f32[22]{0:T(128)S(1)}, f32[22]{0:T(128)S(1)}, u32[]{:S(2)}, u32[]{:S(2)}) collective-permute-start(f32[22]{0:T(128)S(1)} %fusion.28), channel_id=1, source_target_pairs={{0,2},{2,0},{4,6},{6,4},{1,3},{3,1},{5,7},{7,5},{8,10},{10,8},{12,... | collective-permute-start | bytes 272 | tf_op jit(solution)/shard_map/ppermute | solution.py:39
  139.3 5.1 %collective-permute-start.2 = (f32[22]{0:T(128)S(1)}, f32[22]{0:T(128)S(1)}, u32[]{:S(2)}, u32[]{:S(2)}) collective-permute-start(f32[22]{0:T(128)S(1)} %add.138), channel_id=1, source_target_pairs={{0,4},{2,6},{4,0},{6,2},{1,5},{3,7},{5,1},{7,3},{8,12},{10,14},{12... | collective-permute-start | bytes 272 | tf_op jit(solution)/shard_map/ppermute | solution.py:39
  144.4 3.6 %collective-permute-start.3 = (f32[22]{0:T(128)S(1)}, f32[22]{0:T(128)S(1)}, u32[]{:S(2)}, u32[]{:S(2)}) collective-permute-start(f32[22]{0:T(128)S(1)} %add.139), channel_id=1, source_target_pairs={{0,8},{8,0},{16,24},{24,16},{32,40},{40,32},{48,56},{56,48},{64,72... | collective-permute-start | bytes 272 | tf_op jit(solution)/shard_map/ppermute | solution.py:39
  148.0 5.1 %collective-permute-start.4 = (f32[22]{0:T(128)S(1)}, f32[22]{0:T(128)S(1)}, u32[]{:S(2)}, u32[]{:S(2)}) collective-permute-start(f32[22]{0:T(128)S(1)} %add.140), channel_id=1, source_target_pairs={{0,16},{8,24},{16,0},{24,8},{32,48},{40,56},{48,32},{56,40},{64,80... | collective-permute-start | bytes 272 | tf_op jit(solution)/shard_map/ppermute | solution.py:39
  153.0 3.6 %collective-permute-start.5 = (f32[22]{0:T(128)S(1)}, f32[22]{0:T(128)S(1)}, u32[]{:S(2)}, u32[]{:S(2)}) collective-permute-start(f32[22]{0:T(128)S(1)} %add.141), channel_id=1, source_target_pairs={{0,32},{8,40},{16,48},{24,56},{32,0},{40,8},{48,16},{56,24},{64,96... | collective-permute-start | bytes 272 | tf_op jit(solution)/shard_map/ppermute | solution.py:39
  156.6 5.1 %collective-permute-start.6 = (f32[22]{0:T(128)S(1)}, f32[22]{0:T(128)S(1)}, u32[]{:S(2)}, u32[]{:S(2)}) collective-permute-start(f32[22]{0:T(128)S(1)} %add.142), channel_id=1, source_target_pairs={{0,64},{8,72},{16,80},{24,88},{32,96},{40,104},{48,112},{56,120},{... | collective-permute-start | bytes 272 | tf_op jit(solution)/shard_map/ppermute | solution.py:39
  163.9 164.6 %all-gather.9.cloned.1.call-start = ((), (), s32[]{:S(2)}) async-start(), calls=%async_computation.3 | async-start | bytes 3168256 | tf_op jit(solution)/shard_map/all_gather | solution.py:118
  221.5 40.2 %copy-start = (f32[50,3200]{1,0:T(8,128)S(1)}, f32[50,3200]{1,0:T(8,128)}, u32[]{:S(2)}) copy-start(f32[50,3200]{1,0:T(8,128)} %get-tuple-element.41) | copy-start | bytes 1920004
  223.5 1.2 collective-permute-start.7
  226.1 3.6 %collective-permute-start.8 = (f32[2]{0:T(128)S(1)}, f32[2]{0:T(128)S(1)}, u32[]{:S(2)}, u32[]{:S(2)}) collective-permute-start(f32[2]{0:T(128)S(1)} %fusion.29), channel_id=1, source_target_pairs={{0,2},{2,0},{4,6},{6,4},{1,3},{3,1},{5,7},{7,5},{8,10},{10,8},{12,... | collective-permute-start | bytes 32 | tf_op jit(solution)/shard_map/ppermute | solution.py:39
  231.0 5.1 %collective-permute-start.9 = (f32[2]{0:T(128)S(1)}, f32[2]{0:T(128)S(1)}, u32[]{:S(2)}, u32[]{:S(2)}) collective-permute-start(f32[2]{0:T(128)S(1)} %fusion.30), channel_id=1, source_target_pairs={{0,4},{2,6},{4,0},{6,2},{1,5},{3,7},{5,1},{7,3},{8,12},{10,14},{12... | collective-permute-start | bytes 32 | tf_op jit(solution)/shard_map/ppermute | solution.py:39
  236.1 3.6 %collective-permute-start.10 = (f32[2]{0:T(128)S(1)}, f32[2]{0:T(128)S(1)}, u32[]{:S(2)}, u32[]{:S(2)}) collective-permute-start(f32[2]{0:T(128)S(1)} %add.156), channel_id=1, source_target_pairs={{0,8},{8,0},{16,24},{24,16},{32,40},{40,32},{48,56},{56,48},{64,72... | collective-permute-start | bytes 32 | tf_op jit(solution)/shard_map/ppermute | solution.py:39
  239.7 5.1 %collective-permute-start.11 = (f32[2]{0:T(128)S(1)}, f32[2]{0:T(128)S(1)}, u32[]{:S(2)}, u32[]{:S(2)}) collective-permute-start(f32[2]{0:T(128)S(1)} %add.157), channel_id=1, source_target_pairs={{0,16},{8,24},{16,0},{24,8},{32,48},{40,56},{48,32},{56,40},{64,80... | collective-permute-start | bytes 32 | tf_op jit(solution)/shard_map/ppermute | solution.py:39
  244.8 3.6 %collective-permute-start.12 = (f32[2]{0:T(128)S(1)}, f32[2]{0:T(128)S(1)}, u32[]{:S(2)}, u32[]{:S(2)}) collective-permute-start(f32[2]{0:T(128)S(1)} %add.158), channel_id=1, source_target_pairs={{0,32},{8,40},{16,48},{24,56},{32,0},{40,8},{48,16},{56,24},{64,96... | collective-permute-start | bytes 32 | tf_op jit(solution)/shard_map/ppermute | solution.py:39
  248.4 5.1 %collective-permute-start.13 = (f32[2]{0:T(128)S(1)}, f32[2]{0:T(128)S(1)}, u32[]{:S(2)}, u32[]{:S(2)}) collective-permute-start(f32[2]{0:T(128)S(1)} %add.159), channel_id=1, source_target_pairs={{0,64},{8,72},{16,80},{24,88},{32,96},{40,104},{48,112},{56,120},{... | collective-permute-start | bytes 32 | tf_op jit(solution)/shard_map/ppermute | solution.py:39
Sparse Core Ops, SparseCore 0:
  24.2 105.4 reduce-scatter.6
  133.7 85.6 reduce-scatter.8
  221.5 57.9 all-gather.6
  281.5 46.9 all-gather.8

commit v4 on v2

--- a/solution.py
+++ b/solution.py
@@ -66,11 +66,11 @@
     vec_index = lax.axis_index("dp") * owned_vec + lax.iota(jnp.int32, owned_vec)
     masks_vec = segment_masks(vec_index, bounds_vec)
 
-    local_grad = grad_mat.reshape(n_dp, owned_rows, columns).astype(jnp.float32)
-    local_vec = grad_vec.reshape(n_dp, 1, owned_vec).astype(jnp.float32)
-    local_vec = jnp.pad(local_vec, ((0, 0), (0, 0), (0, columns - owned_vec)))
+    local_grad = grad_mat.reshape(n_dp, owned_rows, columns)
+    local_vec = jnp.pad(grad_vec.reshape(n_dp, 1, owned_vec), ((0, 0), (0, 0), (0, columns - owned_vec)))
     payload = jnp.concatenate([local_grad, local_vec], axis=1)
-    summed = lax.optimization_barrier(lax.psum_scatter(payload, "dp", scatter_dimension=0, tiled=True))
+    received = lax.all_to_all(payload, "dp", 0, 0, tiled=True)
+    summed = jnp.sum(received.astype(jnp.float32), axis=0, keepdims=True)
     gradient = summed[0, :owned_rows]
     gradient_v = summed[0, owned_rows, :owned_vec]
 

time: 268 us -> 288 us (1.075)
  waiting for transfers between devices: 189 us -> 207 us
  starting transfers between devices: 12.6 us -> 17.1 us
    all_to_all x0 -> x1, waiting for transfers between devices: none -> 127 us  [local(): received = lax.all_to_all(payload, 'dp', 0, 0, tiled=True)]
    unnamed x3 -> x1, waiting for transfers between devices: 114 us -> 0.02 us
    all_to_all x0 -> x1, starting transfers between devices: none -> 8.17 us  [local(): received = lax.all_to_all(payload, 'dp', 0, 0, tiled=True)]
    convert_element_type x2 -> x0, local copies, waits for them, and re-layouts: 7.98 us -> none  [the longest x1 7.85 us: local(): local_grad = grad_mat.reshape(n_dp, owned_rows, columns).astype(jnp.float32)]
    reshape x0 -> x2, local copies, waits for them, and re-layouts: none -> 7.91 us  [the longest x1 7.78 us: local(): local_grad = grad_mat.reshape(n_dp, owned_rows, columns)]
    reduce_sum x0 -> x1, other arithmetic: none -> 5.07 us  [local(): summed = jnp.sum(received.astype(jnp.float32), axis=0, keepdims=True)]
    ppermute x7, waiting for transfers between devices: 14.5 us -> 18.2 us  [butterfly_sum(): x = x + lax.ppermute(x, axis, [(i, i ^ step) for i in range(size)])]
    ppermute x7, starting transfers between devices: 12.5 us -> 8.86 us  [butterfly_sum(): x = x + lax.ppermute(x, axis, [(i, i ^ step) for i in range(size)])]
  transfers between devices with their start and end apart: 9 -> 9, of which waited for: 9 -> 9; matrix products, arithmetic and copies ran while one was open for 5% -> 4% of each run, Pallas kernels for 0% -> 0%
where the time goes in v4:
time: 288 us; the launch traced here: 287 us
  waiting for transfers between devices  207 us (72%)
  other arithmetic  30.1 us (10%)
  local copies, waits for them, and re-layouts  19.3 us (7%)
  starting transfers between devices  17.1 us (6%)
  between operations  14.3 us (5%)
    all_to_all x1, waiting for transfers between devices, local(): received = lax.all_to_all(payload, 'dp', 0, 0, tiled=True)  127 us
    all_gather x1, waiting for transfers between devices, local(): gathered = lax.all_gather(weights_rows, 'dp', axis=0, tiled=False)  61.5 us
    ppermute x7, waiting for transfers between devices, butterfly_sum(): x = x + lax.ppermute(x, axis, [(i, i ^ step) for i in range(size)])  18.2 us
    unnamed x3, other arithmetic  12.1 us
    ppermute x7, starting transfers between devices, butterfly_sum(): x = x + lax.ppermute(x, axis, [(i, i ^ step) for i in range(size)])  8.86 us
    reshape x1, local copies, waits for them, and re-layouts, local(): weights_mat = gathered[:, :owned_rows].reshape(1, section_rows, columns)  8.78 us
    all_to_all x1, starting transfers between devices, local(): received = lax.all_to_all(payload, 'dp', 0, 0, tiled=True)  8.17 us
    reshape x1, local copies, waits for them, and re-layouts, local(): local_grad = grad_mat.reshape(n_dp, owned_rows, columns)  7.78 us
  transfers between devices with their start and end apart: 9, of which 9 were waited for; matrix products, arithmetic and copies ran while one was open for 4% of the time, Pallas kernels for 0%

profile of v4, /device:TPU:0, one launch (start us, length us, event | category | flops | bytes accessed | tf_op | source)
XLA Modules:
  0.0 287.3 jit_solution(12835606737588881098)
XLA Ops:
  7.2 1.1 reduce
  8.4 7.8 %reshape.142 = bf16[16,50,4800]{2,1,0:T(8,128)(2,1)} reshape(bf16[1,1,800,4800]{3,2,1,0:T(8,128)(2,1)} %param.12) | data formatting | bytes 15360000 | tf_op jit(solution)/shard_map/reshape | solution.py:69
  16.2 7.3 %fusion.1 = bf16[16,51,4800]{2,1,0:T(8,128)(2,1)} fusion(bf16[16,1,1300]{2,1,0:T(2,128)(2,1)S(1)} %reshape.150, bf16[16,50,4800]{2,1,0:T(8,128)(2,1)} %reshape.142), kind=kLoop, calls=%fused_computation.3 | loop fusion | flops 23500800 | bytes 15555200 | tf_op jit(solution)/shard_map/concatenate | solution.py:71
  23.5 8.2 %all-to-all-start = ((bf16[16,51,4800]{2,1,0:T(8,128)(2,1)}), bf16[16,51,4800]{2,1,0:T(8,128)(2,1)}, u32[]{:S(2)}, u32[]{:S(2)}) async-start(bf16[16,51,4800]{2,1,0:T(8,128)(2,1)} %fusion.1), calls=%async_computation | async-start | bytes 17432576 | tf_op jit(solution)/shard_map/all_to_all | solution.py:72
  31.8 1.9 bitcast_multiply_fusion.3
  33.8 126.9 %all-to-all-done = bf16[16,51,4800]{2,1,0:T(8,128)(2,1)} async-done(((bf16[16,51,4800]{2,1,0:T(8,128)(2,1)}), bf16[16,51,4800]{2,1,0:T(8,128)(2,1)}, u32[]{:S(2)}, u32[]{:S(2)}) %all-to-all-start) | async-done | bytes 7833632 | tf_op jit(solution)/shard_map/all_to_all | solution.py:72
  160.6 5.1 %convert_reduce_fusion = f32[51,4800]{1,0:T(8,128)S(1)} fusion(bf16[16,51,4800]{2,1,0:T(8,128)(2,1)} %all-to-all-done), kind=kLoop, calls=%fused_computation.1 | loop fusion | flops 7588800 | bytes 8812800 | tf_op jit(solution)/shard_map/reduce_sum | solution.py:73
  165.7 0.6 multiply_reduce_fusion.1
  166.4 0.2 select_reduce_fusion.5
  166.7 1.0 multiply_reduce_fusion
  167.8 0.3 select_reduce_fusion.2
  168.2 1.1 collective-permute-done
  169.4 1.6 collective-permute-start.1
  171.0 2.0 collective-permute-done.1
  173.0 3.2 %collective-permute-start.2 = (f32[24]{0:T(128)S(1)}, f32[24]{0:T(128)S(1)}, u32[]{:S(2)}, u32[]{:S(2)}) collective-permute-start(f32[24]{0:T(128)S(1)} %add.114), channel_id=1, source_target_pairs={{0,4},{2,6},{4,0},{6,2},{1,5},{3,7},{5,1},{7,3},{8,12},{10,14},{12... | collective-permute-start | bytes 296 | tf_op jit(solution)/shard_map/ppermute | solution.py:39
  176.2 1.9 collective-permute-done.2
  178.1 3.6 %collective-permute-done.3 = f32[24]{0:T(128)S(1)} collective-permute-done((f32[24]{0:T(128)S(1)}, f32[24]{0:T(128)S(1)}, u32[]{:S(2)}, u32[]{:S(2)}) %collective-permute-start.3) | collective-permute-done | bytes 128 | tf_op jit(solution)/shard_map/ppermute | solution.py:39
  181.7 1.3 collective-permute-start.4
  182.9 3.8 %collective-permute-done.4 = f32[24]{0:T(128)S(1)} collective-permute-done((f32[24]{0:T(128)S(1)}, f32[24]{0:T(128)S(1)}, u32[]{:S(2)}, u32[]{:S(2)}) %collective-permute-start.4) | collective-permute-done | bytes 128 | tf_op jit(solution)/shard_map/ppermute | solution.py:39
  186.7 1.0 collective-permute-start.5
  187.7 2.6 collective-permute-done.5
  190.3 1.8 collective-permute-start.6
  192.2 3.2 %collective-permute-done.6 = f32[24]{0:T(128)S(1)} collective-permute-done((f32[24]{0:T(128)S(1)}, f32[24]{0:T(128)S(1)}, u32[]{:S(2)}, u32[]{:S(2)}) %collective-permute-start.6) | collective-permute-done | bytes 128 | tf_op jit(solution)/shard_map/ppermute | solution.py:39
  195.7 0.1 select_reduce_fusion
  196.0 0.9 maximum_bitcast_fusion
  197.0 0.6 multiply_subtract_fusion
  197.6 0.4 copy-done.3
  198.1 10.1 %fusion.14 = (f32[1,1,1,50,4800]{4,2,3,1,0:T(1,128)}, f32[1,1,1,50,4800]{4,0,3,2,1:T(1,128)}, f32[1,1,1,50,4800]{4,2,3,1,0:T(1,128)}) fusion(f32[1,1,1,50,4800]{4,2,3,1,0:T(1,128)S(1)} %copy-done, f32[4800]{0:T(1024)S(1)} %broadcast_multiply_fusion, f32[1,50,4800]{2,1,0:T(8,128)S(1)} %bitcast.70, f32[1,1,1,50,4800]{4,2,3,1,0:T(1,128)S(1)} %copy-done.3, ...), kind=kLoop, calls=%fused_computation.28 | loop fusion | flops 3360000 | bytes 6739200
  208.2 61.5 %all-gather.4.cloned.1.call-done = bf16[16,51,4800]{2,1,0:T(8,128)(2,1)} async-done(((bf16[1,51,4800]{2,1,0:T(8,128)(2,1)}), bf16[16,51,4800]{2,1,0:T(8,128)(2,1)}) %all-gather.4.cloned.1.call-update) | async-done | bytes 7833616 | tf_op jit(solution)/shard_map/all_gather | solution.py:104
  269.7 8.8 %reshape.145 = bf16[1,800,4800]{2,1,0:T(8,128)(2,1)} reshape(bf16[16,50,4800]{2,1,0:T(8,128)(2,1)} %bitcast.71) | data formatting | bytes 15360000 | tf_op jit(solution)/shard_map/reshape | solution.py:105
  278.4 1.3 slice_reduce_fusion
  279.7 0.8 reshape_squeeze.3
  (48 shorter events, 1.1 us)
Async XLA Ops:
  23.5 8.2 %copy-start.2 = (f32[1,1,1,50,4800]{4,2,3,1,0:T(1,128)S(1)}, f32[1,1,1,50,4800]{4,2,3,1,0:T(1,128)}, u32[]{:S(2)}) copy-start(f32[1,1,1,50,4800]{4,2,3,1,0:T(1,128)} %param.15) | copy-start | bytes 2880004
  23.5 137.1 %all-to-all-start = ((bf16[16,51,4800]{2,1,0:T(8,128)(2,1)}), bf16[16,51,4800]{2,1,0:T(8,128)(2,1)}, u32[]{:S(2)}, u32[]{:S(2)}) async-start(bf16[16,51,4800]{2,1,0:T(8,128)(2,1)} %fusion.1), calls=%async_computation | async-start | bytes 17432576 | tf_op jit(solution)/shard_map/all_to_all | solution.py:72
  31.7 238.0 %all-gather.4.cloned.1.call-start = ((), (), s32[]{:S(2)}) async-start(), calls=%async_computation.1 | async-start | bytes 9261056 | tf_op jit(solution)/shard_map/all_gather | solution.py:104
  33.7 132.0 %copy-start.5 = (f32[1,1300]{1,0:T(1,128)S(1)}, f32[1,1300]{1,0:T(1,128)}, u32[]{:S(2)}) copy-start(f32[1,1300]{1,0:T(1,128)} %param.17) | copy-start | bytes 15604
  33.7 132.0 %copy-start.6 = (f32[1,1300]{1,0:T(1,128)S(1)}, f32[1,1300]{1,0:T(1,128)}, u32[]{:S(2)}) copy-start(f32[1,1300]{1,0:T(1,128)} %param.18) | copy-start | bytes 15604
  33.7 132.0 %copy-start.7 = (f32[1,1300]{1,0:T(1,128)S(1)}, f32[1,1300]{1,0:T(1,128)}, u32[]{:S(2)}) copy-start(f32[1,1300]{1,0:T(1,128)} %param.19) | copy-start | bytes 15604
  33.7 132.7 %copy-start.10 = (s32[8]{0:T(128)S(1)}, s32[8]{0:T(128)}, u32[]{:S(2)}) copy-start(s32[8]{0:T(128)} %constant.69.clone) | copy-start | bytes 100
  33.7 132.7 %copy-start.11 = (s32[8]{0:T(128)S(1)}, s32[8]{0:T(128)}, u32[]{:S(2)}) copy-start(s32[8]{0:T(128)} %constant.68.clone) | copy-start | bytes 100
  33.7 133.0 %copy-start = (f32[1,1,1,50,4800]{4,2,3,1,0:T(1,128)S(1)}, f32[1,1,1,50,4800]{4,2,3,1,0:T(1,128)}, u32[]{:S(2)}) copy-start(f32[1,1,1,50,4800]{4,2,3,1,0:T(1,128)} %param.14) | copy-start | bytes 2880004
  33.8 133.0 %copy-start.1 = (f32[1,1,1,50,4800]{4,2,3,1,0:T(1,128)S(1)}, f32[1,1,1,50,4800]{4,2,3,1,0:T(1,128)}, u32[]{:S(2)}) copy-start(f32[1,1,1,50,4800]{4,2,3,1,0:T(1,128)} %param.16) | copy-start | bytes 2880004
  160.6 6.1 %copy-start.4 = (f32[1,1,1,50,4800]{4,0,3,2,1:T(1,128)S(1)}, f32[1,1,1,50,4800]{4,0,3,2,1:T(1,128)}, u32[]{:S(2)}) copy-start(f32[1,1,1,50,4800]{4,0,3,2,1:T(1,128)} %bitcast_multiply_fusion.3) | copy-start | bytes 2880004
  166.7 1.0 copy-start.8
  166.7 1.0 copy-start.9
  168.2 1.2 collective-permute-start
  169.4 3.6 %collective-permute-start.1 = (f32[24]{0:T(128)S(1)}, f32[24]{0:T(128)S(1)}, u32[]{:S(2)}, u32[]{:S(2)}) collective-permute-start(f32[24]{0:T(128)S(1)} %fusion.32), channel_id=1, source_target_pairs={{0,2},{2,0},{4,6},{6,4},{1,3},{3,1},{5,7},{7,5},{8,10},{10,8},{12,... | collective-permute-start | bytes 296 | tf_op jit(solution)/shard_map/ppermute | solution.py:39
  173.0 5.1 %collective-permute-start.2 = (f32[24]{0:T(128)S(1)}, f32[24]{0:T(128)S(1)}, u32[]{:S(2)}, u32[]{:S(2)}) collective-permute-start(f32[24]{0:T(128)S(1)} %add.114), channel_id=1, source_target_pairs={{0,4},{2,6},{4,0},{6,2},{1,5},{3,7},{5,1},{7,3},{8,12},{10,14},{12... | collective-permute-start | bytes 296 | tf_op jit(solution)/shard_map/ppermute | solution.py:39
  178.1 3.6 %collective-permute-start.3 = (f32[24]{0:T(128)S(1)}, f32[24]{0:T(128)S(1)}, u32[]{:S(2)}, u32[]{:S(2)}) collective-permute-start(f32[24]{0:T(128)S(1)} %add.115), channel_id=1, source_target_pairs={{0,8},{8,0},{16,24},{24,16},{32,40},{40,32},{48,56},{56,48},{64,72... | collective-permute-start | bytes 296 | tf_op jit(solution)/shard_map/ppermute | solution.py:39
  181.7 5.1 %collective-permute-start.4 = (f32[24]{0:T(128)S(1)}, f32[24]{0:T(128)S(1)}, u32[]{:S(2)}, u32[]{:S(2)}) collective-permute-start(f32[24]{0:T(128)S(1)} %add.116), channel_id=1, source_target_pairs={{0,16},{8,24},{16,0},{24,8},{32,48},{40,56},{48,32},{56,40},{64,80... | collective-permute-start | bytes 296 | tf_op jit(solution)/shard_map/ppermute | solution.py:39
  186.7 3.6 %collective-permute-start.5 = (f32[24]{0:T(128)S(1)}, f32[24]{0:T(128)S(1)}, u32[]{:S(2)}, u32[]{:S(2)}) collective-permute-start(f32[24]{0:T(128)S(1)} %add.117), channel_id=1, source_target_pairs={{0,32},{8,40},{16,48},{24,56},{32,0},{40,8},{48,16},{56,24},{64,96... | collective-permute-start | bytes 296 | tf_op jit(solution)/shard_map/ppermute | solution.py:39
  190.3 5.1 %collective-permute-start.6 = (f32[24]{0:T(128)S(1)}, f32[24]{0:T(128)S(1)}, u32[]{:S(2)}, u32[]{:S(2)}) collective-permute-start(f32[24]{0:T(128)S(1)} %add.118), channel_id=1, source_target_pairs={{0,64},{8,72},{16,80},{24,88},{32,96},{40,104},{48,112},{56,120},{... | collective-permute-start | bytes 296 | tf_op jit(solution)/shard_map/ppermute | solution.py:39
  196.9 1.2 copy-start.3
Sparse Core Ops, SparseCore 0:
  197.0 72.6 all-gather.3

commit v5 on v1

--- a/solution.py
+++ b/solution.py
@@ -28,6 +28,14 @@
     lower = jnp.array(bounds[:-1], dtype=jnp.int32)[:, None]
     upper = jnp.array(bounds[1:], dtype=jnp.int32)[:, None]
     return ((position[None, :] >= lower) & (position[None, :] < upper)).astype(jnp.float32)
+
+
+def all_sum(x, axes):
+    count = 1
+    for axis in axes:
+        count *= lax.axis_size(axis)
+    copies = jnp.broadcast_to(x[None], (count,) + x.shape)
+    return jnp.sum(lax.all_to_all(copies, axes, 0, 0, tiled=True), axis=0)
 
 
 def local(grad_mat, grad_vec, master_mat, first_mat, second_mat, master_vec, first_vec, second_vec):
@@ -76,7 +84,7 @@
 
     vec_owner = (lax.axis_index("tensor") == 0) & (lax.axis_index("section") == 0)
     vec_part = jnp.where(vec_owner, jnp.concatenate([weight_vec_sq, update_vec_sq]), 0.0)
-    sums = lax.psum(jnp.concatenate([weight_mat_sq, update_mat_sq, vec_part]), ("dp", "tensor", "section"))
+    sums = all_sum(jnp.concatenate([weight_mat_sq, update_mat_sq, vec_part]), ("dp", "tensor", "section"))
     n_mat = weight_mat_sq.shape[0]
     n_vec = weight_vec_sq.shape[0]
     wsum_mat, usum_mat = sums[:n_mat], sums[n_mat : 2 * n_mat]

time: 303 us -> 255 us (0.84)
  blocking collectives: 64.3 us -> 0 us
  starting transfers between devices: 0.08 us -> 8.18 us
  waiting for transfers between devices: 172 us -> 180 us
    psum x1 -> x0, blocking collectives: 64.3 us -> none  [local(): lax.psum(jnp.concatenate([weight_mat_sq, update_mat_sq, vec_part]), ('dp'...]
    all_to_all x0 -> x1, waiting for transfers between devices: none -> 9.17 us  [all_sum(): return jnp.sum(lax.all_to_all(copies, axes, 0, 0, tiled=True), axis=0)]
    all_to_all x0 -> x1, starting transfers between devices: none -> 8.1 us  [all_sum(): return jnp.sum(lax.all_to_all(copies, axes, 0, 0, tiled=True), axis=0)]
  transfers between devices with their start and end apart: 2 -> 3, of which waited for: 2 -> 3; matrix products, arithmetic and copies ran while one was open for 4% -> 5% of each run, Pallas kernels for 0% -> 0%
where the time goes in v5:
time: 255 us; the launch traced here: 254 us
  waiting for transfers between devices  180 us (71%)
  other arithmetic  30.3 us (12%)
  local copies, waits for them, and re-layouts  21.6 us (8%)
  between operations  14.2 us (6%)
  starting transfers between devices  8.18 us (3%)
    unnamed x3, waiting for transfers between devices  114 us
    all_gather x1, waiting for transfers between devices, local(): gathered = lax.all_gather(weights_rows, 'dp', axis=0, tiled=False)  56.9 us
    unnamed x3, other arithmetic  11.2 us
    concatenate x1, other arithmetic, local(): payload = jnp.concatenate([local_grad, local_vec], axis=1)  10.7 us
    all_to_all x1, waiting for transfers between devices, all_sum(): return jnp.sum(lax.all_to_all(copies, axes, 0, 0, tiled=True), axis=0)  9.17 us
    reshape x1, local copies, waits for them, and re-layouts, local(): weights_mat = gathered[:, :owned_rows].reshape(1, section_rows, columns)  8.78 us
    all_to_all x1, starting transfers between devices, all_sum(): return jnp.sum(lax.all_to_all(copies, axes, 0, 0, tiled=True), axis=0)  8.1 us
    convert_element_type x1, local copies, waits for them, and re-layouts, local(): local_grad = grad_mat.reshape(n_dp, owned_rows, columns).astype(jnp.float32)  7.85 us
  transfers between devices with their start and end apart: 3, of which 3 were waited for; matrix products, arithmetic and copies ran while one was open for 5% of the time, Pallas kernels for 0%

profile of v5, /device:TPU:0, one launch (start us, length us, event | category | flops | bytes accessed | tf_op | source)
XLA Modules:
  0.0 254.4 jit_solution(8058954195357774736)
XLA Ops:
  7.2 7.8 %convert_element_type.28 = bf16[16,50,4800]{2,1,0:T(8,128)(2,1)} reshape(bf16[1,1,800,4800]{3,2,1,0:T(8,128)(2,1)} %param.12) | data formatting | bytes 15360000 | tf_op jit(solution)/shard_map/convert_element_type | solution.py:66
  15.1 0.2 reduce.1
  15.3 0.1 convert_element_type.32
  15.4 10.7 %fusion.2 = f32[16,51,4800]{2,1,0:T(8,128)} fusion(bf16[16,1,1300]{2,1,0:T(2,128)(2,1)S(1)} %convert_element_type.32, bf16[16,50,4800]{2,1,0:T(8,128)(2,1)} %convert_element_type.28), kind=kLoop, calls=%fused_computation.3 | loop fusion | flops 23500800 | bytes 23388800 | tf_op jit(solution)/shard_map/concatenate | solution.py:69
  26.3 1.1 copy-done.3
  27.4 1.9 bitcast_multiply_fusion.3
  29.3 114.0 %reduce-scatter.4.cloned.1.call-done = f32[1,51,4800]{2,1,0:T(8,128)} async-done(((f32[16,51,4800]{2,1,0:T(8,128)}), f32[1,51,4800]{2,1,0:T(8,128)}) %reduce-scatter.4.cloned.1.call-update) | async-done | bytes 979216
  143.3 1.4 multiply_reduce_fusion.1
  144.8 0.2 select_reduce_fusion.5
  145.0 0.1 broadcast_select_fusion
  145.1 2.9 %multiply_reduce_fusion = (f32[4800]{0:T(1024)S(1)}, f32[50,4800]{1,0:T(8,128)S(1)}, f32[4800]{0:T(1024)S(1)}) fusion(f32[1,1,1,50,4800]{4,2,3,1,0:T(1,128)S(1)} %copy-done, f32[1,1,1,50,4800]{4,2,3,1,0:T(1,128)} %param.16, f32[1,51,4800]{2,1,0:T(8,128)} %reduce-scatter.4.cloned.1.call-done, f32[1,1,1,50,4800]{4,0,3,2,1:T(1,128)} %bitcast_multiply_fusion.3), kind=kLoop, calls=%fused_computation.21 | loop fusion | flops 3830400 | bytes 4838400 | tf_op jit(solution)/shard_map/reduce_sum | solution.py:82
  148.0 0.3 select_reduce_fusion.2
  148.3 0.1 pad_maximum_fusion
  148.4 0.7 broadcast_in_dim.8
  149.1 8.1 %all-to-all-start = ((f32[128,1,24]{2,1,0:T(1,128)}), f32[128,1,24]{2,1,0:T(1,128)S(1)}, u32[]{:S(2)}, u32[]{:S(2)}) async-start(f32[128,1,24]{2,1,0:T(1,128)} %broadcast_in_dim.8), calls=%async_computation | async-start | bytes 131072 | tf_op jit(solution)/shard_map/all_to_all | solution.py:38
  157.3 9.2 %all-to-all-done = f32[128,1,24]{2,1,0:T(1,128)S(1)} async-done(((f32[128,1,24]{2,1,0:T(1,128)}), f32[128,1,24]{2,1,0:T(1,128)S(1)}, u32[]{:S(2)}, u32[]{:S(2)}) %all-to-all-start) | async-done | bytes 12320 | tf_op jit(solution)/shard_map/all_to_all | solution.py:38
  166.5 0.2 reduce_sum.87
  166.6 0.1 rsqrt_multiply_fusion
  166.7 0.1 rsqrt_multiply_fusion.1
  166.8 0.1 select_reduce_fusion.3
  166.9 0.1 select_reduce_fusion
  167.1 0.1 fusion.11
  167.2 0.9 maximum_bitcast_fusion
  168.1 0.5 copy-done.2
  168.6 0.1 copy_multiply_fusion
  168.8 0.6 multiply_subtract_fusion
  169.4 0.5 copy-done.4
  169.8 10.1 %fusion.15 = (f32[1,1,1,50,4800]{4,2,3,1,0:T(1,128)}, f32[1,1,1,50,4800]{4,0,3,2,1:T(1,128)}, f32[1,1,1,50,4800]{4,2,3,1,0:T(1,128)}) fusion(f32[1,1,1,50,4800]{4,2,3,1,0:T(1,128)S(1)} %copy-done, f32[4800]{0:T(1024)S(1)} %broadcast_multiply_fusion, f32[1,50,4800]{2,1,0:T(8,128)S(1)} %bitcast.68, f32[1,1,1,50,4800]{4,2,3,1,0:T(1,128)S(1)} %copy-done.4, ...), kind=kLoop, calls=%fused_computation.28 | loop fusion | flops 3360000 | bytes 6739200
  179.9 56.9 %all-gather.4.cloned.1.call-done = bf16[16,51,4800]{2,1,0:T(8,128)(2,1)} async-done(((bf16[1,51,4800]{2,1,0:T(8,128)(2,1)}), bf16[16,51,4800]{2,1,0:T(8,128)(2,1)}) %all-gather.4.cloned.1.call-update) | async-done | bytes 7833616 | tf_op jit(solution)/shard_map/all_gather | solution.py:101
  236.8 8.8 %reshape.161 = bf16[1,800,4800]{2,1,0:T(8,128)(2,1)} reshape(bf16[16,50,4800]{2,1,0:T(8,128)(2,1)} %bitcast.67) | data formatting | bytes 15360000 | tf_op jit(solution)/shard_map/reshape | solution.py:102
  245.6 1.3 slice_reduce_fusion
  246.8 0.8 reshape_squeeze.3
  (33 shorter events, 0.3 us)
Async XLA Ops:
  7.2 7.9 %copy-start.5 = (bf16[1,20800]{1,0:T(2,128)(2,1)S(1)}, bf16[1,20800]{1,0:T(2,128)(2,1)}, u32[]{:S(2)}) copy-start(bf16[1,20800]{1,0:T(2,128)(2,1)} %param.13) | copy-start | bytes 124804
  7.2 136.2 %reduce-scatter.4.cloned.1.call-start = ((), (), s32[]{:S(2)}) async-start(), calls=%async_computation.3 | async-start | bytes 18522112
  26.2 1.2 copy-start.3
  26.2 117.1 %copy-start.6 = (f32[1,1300]{1,0:T(1,128)S(1)}, f32[1,1300]{1,0:T(1,128)}, u32[]{:S(2)}) copy-start(f32[1,1300]{1,0:T(1,128)} %param.17) | copy-start | bytes 15604
  26.2 117.1 %copy-start.7 = (f32[1,1300]{1,0:T(1,128)S(1)}, f32[1,1300]{1,0:T(1,128)}, u32[]{:S(2)}) copy-start(f32[1,1300]{1,0:T(1,128)} %param.18) | copy-start | bytes 15604
  26.2 117.1 %copy-start.8 = (f32[1,1300]{1,0:T(1,128)S(1)}, f32[1,1300]{1,0:T(1,128)}, u32[]{:S(2)}) copy-start(f32[1,1300]{1,0:T(1,128)} %param.19) | copy-start | bytes 15604
  26.2 118.5 %copy-start.11 = (s32[8]{0:T(128)S(1)}, s32[8]{0:T(128)}, u32[]{:S(2)}) copy-start(s32[8]{0:T(128)} %constant.70.clone) | copy-start | bytes 100
  26.2 118.5 %copy-start.12 = (s32[8]{0:T(128)S(1)}, s32[8]{0:T(128)}, u32[]{:S(2)}) copy-start(s32[8]{0:T(128)} %constant.71.clone) | copy-start | bytes 100
  26.3 118.8 %copy-start = (f32[1,1,1,50,4800]{4,2,3,1,0:T(1,128)S(1)}, f32[1,1,1,50,4800]{4,2,3,1,0:T(1,128)}, u32[]{:S(2)}) copy-start(f32[1,1,1,50,4800]{4,2,3,1,0:T(1,128)} %param.14) | copy-start | bytes 2880004
  145.1 2.9 %copy-start.9 = (s32[4]{0:T(128)S(1)}, s32[4]{0:T(128)}, u32[]{:S(2)}) copy-start(s32[4]{0:T(128)} %constant.68.clone) | copy-start | bytes 52
  145.1 2.9 %copy-start.10 = (s32[4]{0:T(128)S(1)}, s32[4]{0:T(128)}, u32[]{:S(2)}) copy-start(s32[4]{0:T(128)} %constant.69.clone) | copy-start | bytes 52
  145.1 12.2 %copy-start.1 = (f32[1,51,4800]{2,1,0:T(8,128)S(1)}, f32[1,51,4800]{2,1,0:T(8,128)}, u32[]{:S(2)}) copy-start(f32[1,51,4800]{2,1,0:T(8,128)} %reduce-scatter.4.cloned.1.call-done) | copy-start | bytes 2937604
  149.1 17.4 %all-to-all-start = ((f32[128,1,24]{2,1,0:T(1,128)}), f32[128,1,24]{2,1,0:T(1,128)S(1)}, u32[]{:S(2)}, u32[]{:S(2)}) async-start(f32[128,1,24]{2,1,0:T(1,128)} %broadcast_in_dim.8), calls=%async_computation | async-start | bytes 131072 | tf_op jit(solution)/shard_map/all_to_all | solution.py:38
  157.2 79.6 %all-gather.4.cloned.1.call-start = ((), (), s32[]{:S(2)}) async-start(), calls=%async_computation.2 | async-start | bytes 9261056 | tf_op jit(solution)/shard_map/all_gather | solution.py:101
  167.2 1.4 copy-start.2
  168.6 1.2 copy-start.4
Sparse Core Ops, SparseCore 0:
  26.3 116.9 reduce-scatter.3
  168.2 68.4 all-gather.3

commit v6 on v5

--- a/solution.py
+++ b/solution.py
@@ -2,6 +2,8 @@
 import jax.numpy as jnp
 from jax import lax
 from jax.sharding import PartitionSpec as P
+from jax.experimental import pallas as pl
+from jax.experimental.pallas import tpu as pltpu
 
 D = 1600
 FF = 6400
@@ -38,6 +40,29 @@
     return jnp.sum(lax.all_to_all(copies, axes, 0, 0, tiled=True), axis=0)
 
 
+def regroup_kernel(owned_rows, rows_ref, vec_ref, out_ref):
+    for j in range(out_ref.shape[0]):
+        out_ref[j, :owned_rows, :] = rows_ref[j * owned_rows : (j + 1) * owned_rows, :].astype(jnp.float32)
+        out_ref[j, owned_rows:, :] = vec_ref[j : j + 1, :]
+
+
+def regroup(rows, vec_rows, n_owners, owned_rows):
+    columns = rows.shape[1]
+    per_step = 8
+    assert n_owners % per_step == 0
+    return pl.pallas_call(
+        lambda r, v, o: regroup_kernel(owned_rows, r, v, o),
+        grid=(n_owners // per_step,),
+        in_specs=[
+            pl.BlockSpec((per_step * owned_rows, columns), lambda i: (i, 0)),
+            pl.BlockSpec((per_step, columns), lambda i: (i, 0)),
+        ],
+        out_specs=pl.BlockSpec((per_step, owned_rows + 1, columns), lambda i: (i, 0, 0)),
+        out_shape=jax.ShapeDtypeStruct((n_owners, owned_rows + 1, columns), jnp.float32),
+        compiler_params=pltpu.CompilerParams(vmem_limit_bytes=48 * 1024 * 1024),
+    )(rows, vec_rows)
+
+
 def local(grad_mat, grad_vec, master_mat, first_mat, second_mat, master_vec, first_vec, second_vec):
     n_dp = lax.axis_size("dp")
     tensor_count = lax.axis_size("tensor")
@@ -63,10 +88,8 @@
     vec_index = lax.axis_index("dp") * owned_vec + lax.iota(jnp.int32, owned_vec)
     masks_vec = segment_masks(vec_index, bounds_vec)
 
-    local_grad = grad_mat.reshape(n_dp, owned_rows, columns).astype(jnp.float32)
-    local_vec = grad_vec.reshape(n_dp, 1, owned_vec).astype(jnp.float32)
-    local_vec = jnp.pad(local_vec, ((0, 0), (0, 0), (0, columns - owned_vec)))
-    payload = jnp.concatenate([local_grad, local_vec], axis=1)
+    local_vec = jnp.pad(grad_vec.reshape(n_dp, owned_vec).astype(jnp.float32), ((0, 0), (0, columns - owned_vec)))
+    payload = regroup(grad_mat.reshape(section_rows, columns), local_vec, n_dp, owned_rows)
     summed = lax.optimization_barrier(lax.psum_scatter(payload, "dp", scatter_dimension=0, tiled=True))
     gradient = summed[0, :owned_rows]
     gradient_v = summed[0, owned_rows, :owned_vec]

time: 255 us -> 247 us (0.969)
  other arithmetic: 30.3 us -> 10.4 us
  Pallas kernels: 0 us -> 8.84 us
  waiting for transfers between devices: 180 us -> 186 us
  local copies, waits for them, and re-layouts: 21.6 us -> 18 us
    concatenate x1 -> x0, other arithmetic: 10.7 us -> none  [local(): payload = jnp.concatenate([local_grad, local_vec], axis=1)]
    unnamed x3 -> x2, other arithmetic: 11.2 us -> 1.98 us
    pallas_call x0 -> x1, Pallas kernels: none -> 8.84 us  [regroup(): pl.pallas_call(lambda r, v, o: regroup_kernel(owned_rows, r, v, o), grid=...]
    convert_element_type x2 -> x1, local copies, waits for them, and re-layouts: 7.98 us -> 0.13 us  [local(): grad_vec.reshape(n_dp, owned_vec).astype(jnp.float32)]
    unnamed x26 -> x23, local copies, waits for them, and re-layouts: 2.11 us -> 6.37 us
    unnamed x3, waiting for transfers between devices: 114 us -> 117 us
    all_gather x1, waiting for transfers between devices: 56.9 us -> 59.7 us  [local(): gathered = lax.all_gather(weights_rows, 'dp', axis=0, tiled=False)]
  transfers between devices with their start and end apart: 3 -> 3, of which waited for: 3 -> 3; matrix products, arithmetic and copies ran while one was open for 5% -> 3% of each run, Pallas kernels for 0% -> 0%
where the time goes in v6:
time: 247 us; the launch traced here: 246 us
  waiting for transfers between devices  186 us (75%)
  local copies, waits for them, and re-layouts  18 us (7%)
  between operations  14.2 us (6%)
  other arithmetic  10.4 us (4%)
  Pallas kernels  8.84 us (4%)
  starting transfers between devices  8.18 us (3%)
    unnamed x3, waiting for transfers between devices  117 us
    all_gather x1, waiting for transfers between devices, local(): gathered = lax.all_gather(weights_rows, 'dp', axis=0, tiled=False)  59.7 us
    all_to_all x1, waiting for transfers between devices, all_sum(): return jnp.sum(lax.all_to_all(copies, axes, 0, 0, tiled=True), axis=0)  9.17 us
    pallas_call x1, Pallas kernels, regroup(): pl.pallas_call(lambda r, v, o: regroup_kernel(owned_rows, r, v, o), grid=...  8.84 us
    reshape x1, local copies, waits for them, and re-layouts, local(): weights_mat = gathered[:, :owned_rows].reshape(1, section_rows, columns)  8.78 us
    all_to_all x1, starting transfers between devices, all_sum(): return jnp.sum(lax.all_to_all(copies, axes, 0, 0, tiled=True), axis=0)  8.1 us
    unnamed x23, local copies, waits for them, and re-layouts  6.37 us
  transfers between devices with their start and end apart: 3, of which 3 were waited for; matrix products, arithmetic and copies ran while one was open for 3% of the time, Pallas kernels for 0%

profile of v6, /device:TPU:0, one launch (start us, length us, event | category | flops | bytes accessed | tf_op | source)
XLA Modules:
  0.0 245.7 jit_solution(17499612240053374059)
XLA Ops:
  7.2 0.0 reduce-scatter.4.cloned.1.call-start
  7.2 1.1 reduce.1
  8.3 0.1 convert_element_type.16
  8.5 8.8 %shard_map.179 = f32[16,51,4800]{2,1,0:T(8,128)} custom-call(bf16[800,4800]{1,0:T(8,128)(2,1)} %bitcast.47, f32[16,4800]{1,0:T(8,128)S(1)} %pad_convert_fusion.v), custom_call_target="tpu_custom_call" | custom-call | tf_op jit(solution)/shard_map/pallas_call | solution.py:53
  17.4 117.1 %reduce-scatter.4.cloned.1.call-done = f32[1,51,4800]{2,1,0:T(8,128)} async-done(((f32[16,51,4800]{2,1,0:T(8,128)}), f32[1,51,4800]{2,1,0:T(8,128)}) %reduce-scatter.4.cloned.1.call-update) | async-done | bytes 979216
  134.5 1.4 multiply_reduce_fusion.1
  136.0 0.2 select_reduce_fusion.5
  136.2 0.1 broadcast_select_fusion
  136.3 3.0 %multiply_reduce_fusion = (f32[4800]{0:T(1024)S(1)}, f32[50,4800]{1,0:T(8,128)S(1)}, f32[4800]{0:T(1024)S(1)}) fusion(f32[1,1,1,50,4800]{4,2,3,1,0:T(1,128)S(1)} %copy-done, f32[1,1,1,50,4800]{4,2,3,1,0:T(1,128)} %param.16, f32[1,51,4800]{2,1,0:T(8,128)} %reduce-scatter.4.cloned.1.call-done, f32[1,1,1,50,4800]{4,2,3,1,0:T(1,128)} %param.15), kind=kLoop, calls=%fused_computation.22 | loop fusion | flops 4070400 | bytes 4838400 | tf_op jit(solution)/shard_map/reduce_sum | solution.py:105
  139.3 0.3 select_reduce_fusion.2
  139.6 0.1 pad_maximum_fusion
  139.7 0.7 broadcast_in_dim.8
  140.4 8.1 %all-to-all-start = ((f32[128,1,24]{2,1,0:T(1,128)}), f32[128,1,24]{2,1,0:T(1,128)S(1)}, u32[]{:S(2)}, u32[]{:S(2)}) async-start(f32[128,1,24]{2,1,0:T(1,128)} %broadcast_in_dim.8), calls=%async_computation | async-start | bytes 131072 | tf_op jit(solution)/shard_map/all_to_all | solution.py:40
  148.5 0.0 all-gather.4.cloned.1.call-start
  148.6 9.2 %all-to-all-done = f32[128,1,24]{2,1,0:T(1,128)S(1)} async-done(((f32[128,1,24]{2,1,0:T(1,128)}), f32[128,1,24]{2,1,0:T(1,128)S(1)}, u32[]{:S(2)}, u32[]{:S(2)}) %all-to-all-start) | async-done | bytes 12320 | tf_op jit(solution)/shard_map/all_to_all | solution.py:40
  157.7 0.2 reduce_sum.87
  157.9 0.1 rsqrt_multiply_fusion
  158.0 0.1 rsqrt_multiply_fusion.1
  158.0 0.1 select_reduce_fusion.3
  158.2 0.1 select_reduce_fusion
  158.3 0.1 fusion.8
  158.5 0.9 maximum_bitcast_fusion
  159.4 0.5 copy-done.2
  159.9 2.0 multiply_subtract_fusion
  161.9 1.9 copy.53
  163.9 1.9 copy.54
  165.8 1.9 copy.55
  167.7 0.6 multiply_subtract_fusion.1
  168.3 59.7 %all-gather.4.cloned.1.call-done = bf16[16,51,4800]{2,1,0:T(8,128)(2,1)} async-done(((bf16[1,51,4800]{2,1,0:T(8,128)(2,1)}), bf16[16,51,4800]{2,1,0:T(8,128)(2,1)}) %all-gather.4.cloned.1.call-update) | async-done | bytes 7833616 | tf_op jit(solution)/shard_map/all_gather | solution.py:124
  228.0 8.8 %reshape.150 = bf16[1,800,4800]{2,1,0:T(8,128)(2,1)} reshape(bf16[16,50,4800]{2,1,0:T(8,128)(2,1)} %bitcast.46) | data formatting | bytes 15360000 | tf_op jit(solution)/shard_map/reshape | solution.py:125
  236.8 1.3 slice_reduce_fusion
  238.1 0.8 reshape_squeeze.3
  (28 shorter events, 0.2 us)
Async XLA Ops:
  7.2 127.4 %reduce-scatter.4.cloned.1.call-start = ((), (), s32[]{:S(2)}) async-start(), calls=%async_computation.3 | async-start | bytes 18522112
  17.3 117.2 %copy-start.3 = (f32[1,1300]{1,0:T(1,128)S(1)}, f32[1,1300]{1,0:T(1,128)}, u32[]{:S(2)}) copy-start(f32[1,1300]{1,0:T(1,128)} %param.17) | copy-start | bytes 15604
  17.3 117.2 %copy-start.4 = (f32[1,1300]{1,0:T(1,128)S(1)}, f32[1,1300]{1,0:T(1,128)}, u32[]{:S(2)}) copy-start(f32[1,1300]{1,0:T(1,128)} %param.18) | copy-start | bytes 15604
  17.3 117.2 %copy-start.5 = (f32[1,1300]{1,0:T(1,128)S(1)}, f32[1,1300]{1,0:T(1,128)}, u32[]{:S(2)}) copy-start(f32[1,1300]{1,0:T(1,128)} %param.19) | copy-start | bytes 15604
  17.4 118.6 %copy-start.8 = (s32[8]{0:T(128)S(1)}, s32[8]{0:T(128)}, u32[]{:S(2)}) copy-start(s32[8]{0:T(128)} %constant.70.clone) | copy-start | bytes 100
  17.4 118.6 %copy-start.9 = (s32[8]{0:T(128)S(1)}, s32[8]{0:T(128)}, u32[]{:S(2)}) copy-start(s32[8]{0:T(128)} %constant.71.clone) | copy-start | bytes 100
  17.4 118.9 %copy-start = (f32[1,1,1,50,4800]{4,2,3,1,0:T(1,128)S(1)}, f32[1,1,1,50,4800]{4,2,3,1,0:T(1,128)}, u32[]{:S(2)}) copy-start(f32[1,1,1,50,4800]{4,2,3,1,0:T(1,128)} %param.14) | copy-start | bytes 2880004
  136.3 3.0 %copy-start.6 = (s32[4]{0:T(128)S(1)}, s32[4]{0:T(128)}, u32[]{:S(2)}) copy-start(s32[4]{0:T(128)} %constant.68.clone) | copy-start | bytes 52
  136.3 3.0 %copy-start.7 = (s32[4]{0:T(128)S(1)}, s32[4]{0:T(128)}, u32[]{:S(2)}) copy-start(s32[4]{0:T(128)} %constant.69.clone) | copy-start | bytes 52
  136.3 12.2 %copy-start.1 = (f32[1,51,4800]{2,1,0:T(8,128)S(1)}, f32[1,51,4800]{2,1,0:T(8,128)}, u32[]{:S(2)}) copy-start(f32[1,51,4800]{2,1,0:T(8,128)} %reduce-scatter.4.cloned.1.call-done) | copy-start | bytes 2937604
  140.4 17.4 %all-to-all-start = ((f32[128,1,24]{2,1,0:T(1,128)}), f32[128,1,24]{2,1,0:T(1,128)S(1)}, u32[]{:S(2)}, u32[]{:S(2)}) async-start(f32[128,1,24]{2,1,0:T(1,128)} %broadcast_in_dim.8), calls=%async_computation | async-start | bytes 131072 | tf_op jit(solution)/shard_map/all_to_all | solution.py:40
  148.5 79.6 %all-gather.4.cloned.1.call-start = ((), (), s32[]{:S(2)}) async-start(), calls=%async_computation.2 | async-start | bytes 9261056 | tf_op jit(solution)/shard_map/all_gather | solution.py:124
  158.5 1.4 copy-start.2
Sparse Core Ops, SparseCore 0:
  17.5 116.9 reduce-scatter.3
  159.5 68.4 all-gather.3

commit v7 on v6

--- a/solution.py
+++ b/solution.py
@@ -63,6 +63,25 @@
     )(rows, vec_rows)
 
 
+def ungroup_kernel(owned_rows, in_ref, out_ref):
+    for j in range(in_ref.shape[0]):
+        out_ref[j * owned_rows : (j + 1) * owned_rows, :] = in_ref[j, :owned_rows, :]
+
+
+def ungroup(gathered, owned_rows):
+    n_owners, _, columns = gathered.shape
+    per_step = 8
+    assert n_owners % per_step == 0
+    return pl.pallas_call(
+        lambda i, o: ungroup_kernel(owned_rows, i, o),
+        grid=(n_owners // per_step,),
+        in_specs=[pl.BlockSpec((per_step, gathered.shape[1], columns), lambda i: (i, 0, 0))],
+        out_specs=pl.BlockSpec((per_step * owned_rows, columns), lambda i: (i, 0)),
+        out_shape=jax.ShapeDtypeStruct((n_owners * owned_rows, columns), gathered.dtype),
+        compiler_params=pltpu.CompilerParams(vmem_limit_bytes=48 * 1024 * 1024),
+    )(gathered)
+
+
 def local(grad_mat, grad_vec, master_mat, first_mat, second_mat, master_vec, first_vec, second_vec):
     n_dp = lax.axis_size("dp")
     tensor_count = lax.axis_size("tensor")
@@ -122,7 +141,7 @@
     weights_v_row = jnp.pad(master_v_new.astype(jnp.bfloat16), (0, columns - owned_vec))[None, :]
     weights_rows = jnp.concatenate([master_new.astype(jnp.bfloat16), weights_v_row], axis=0)
     gathered = lax.all_gather(weights_rows, "dp", axis=0, tiled=False)
-    weights_mat = gathered[:, :owned_rows].reshape(1, section_rows, columns)
+    weights_mat = ungroup(gathered, owned_rows).reshape(1, section_rows, columns)
     weights_vec = gathered[:, owned_rows, :owned_vec].reshape(vec_length)
     return (
         weights_mat,

time: 247 us -> 244 us (0.988)
  local copies, waits for them, and re-layouts: 18 us -> 9.25 us
  Pallas kernels: 8.84 us -> 14.8 us
    reshape x1 -> x0, local copies, waits for them, and re-layouts: 8.78 us -> none  [local(): weights_mat = gathered[:, :owned_rows].reshape(1, section_rows, columns)]
    pallas_call x0 -> x1, Pallas kernels: none -> 5.93 us  [ungroup(): pl.pallas_call(lambda i, o: ungroup_kernel(owned_rows, i, o), grid=(n_own...]
where the time goes in v7:
time: 244 us; the launch traced here: 243 us
  waiting for transfers between devices  186 us (76%)
  Pallas kernels  14.8 us (6%)
  between operations  14.2 us (6%)
  other arithmetic  10.4 us (4%)
  local copies, waits for them, and re-layouts  9.25 us (4%)
  starting transfers between devices  8.18 us (3%)
    unnamed x3, waiting for transfers between devices  117 us
    all_gather x1, waiting for transfers between devices, local(): gathered = lax.all_gather(weights_rows, 'dp', axis=0, tiled=False)  59.7 us
    all_to_all x1, waiting for transfers between devices, all_sum(): return jnp.sum(lax.all_to_all(copies, axes, 0, 0, tiled=True), axis=0)  9.17 us
    pallas_call x1, Pallas kernels, regroup(): pl.pallas_call(lambda r, v, o: regroup_kernel(owned_rows, r, v, o), grid=...  8.84 us
    all_to_all x1, starting transfers between devices, all_sum(): return jnp.sum(lax.all_to_all(copies, axes, 0, 0, tiled=True), axis=0)  8.1 us
    unnamed x23, local copies, waits for them, and re-layouts  6.37 us
    pallas_call x1, Pallas kernels, ungroup(): pl.pallas_call(lambda i, o: ungroup_kernel(owned_rows, i, o), grid=(n_own...  5.93 us
  transfers between devices with their start and end apart: 3, of which 3 were waited for; matrix products, arithmetic and copies ran while one was open for 3% of the time, Pallas kernels for 0%

profile of v7, /device:TPU:0, one launch (start us, length us, event | category | flops | bytes accessed | tf_op | source)
XLA Modules:
  0.0 242.8 jit_solution(8050224715402223364)
XLA Ops:
  7.2 0.0 reduce-scatter.4.cloned.1.call-start
  7.2 1.1 reduce.1
  8.3 0.1 convert_element_type.16
  8.5 8.8 %shard_map.179 = f32[16,51,4800]{2,1,0:T(8,128)} custom-call(bf16[800,4800]{1,0:T(8,128)(2,1)} %bitcast.47, f32[16,4800]{1,0:T(8,128)S(1)} %pad_convert_fusion.v), custom_call_target="tpu_custom_call" | custom-call | tf_op jit(solution)/shard_map/pallas_call | solution.py:53
  17.4 117.1 %reduce-scatter.4.cloned.1.call-done = f32[1,51,4800]{2,1,0:T(8,128)} async-done(((f32[16,51,4800]{2,1,0:T(8,128)}), f32[1,51,4800]{2,1,0:T(8,128)}) %reduce-scatter.4.cloned.1.call-update) | async-done | bytes 979216
  134.5 1.4 multiply_reduce_fusion.1
  136.0 0.2 select_reduce_fusion.5
  136.2 0.1 broadcast_select_fusion
  136.3 3.0 %multiply_reduce_fusion = (f32[4800]{0:T(1024)S(1)}, f32[50,4800]{1,0:T(8,128)S(1)}, f32[4800]{0:T(1024)S(1)}) fusion(f32[1,1,1,50,4800]{4,2,3,1,0:T(1,128)S(1)} %copy-done, f32[1,1,1,50,4800]{4,2,3,1,0:T(1,128)} %param.16, f32[1,51,4800]{2,1,0:T(8,128)} %reduce-scatter.4.cloned.1.call-done, f32[1,1,1,50,4800]{4,2,3,1,0:T(1,128)} %param.15), kind=kLoop, calls=%fused_computation.22 | loop fusion | flops 4070400 | bytes 4838400 | tf_op jit(solution)/shard_map/reduce_sum | solution.py:124
  139.3 0.3 select_reduce_fusion.2
  139.6 0.1 pad_maximum_fusion
  139.7 0.7 broadcast_in_dim.8
  140.4 8.1 %all-to-all-start = ((f32[128,1,24]{2,1,0:T(1,128)}), f32[128,1,24]{2,1,0:T(1,128)S(1)}, u32[]{:S(2)}, u32[]{:S(2)}) async-start(f32[128,1,24]{2,1,0:T(1,128)} %broadcast_in_dim.8), calls=%async_computation | async-start | bytes 131072 | tf_op jit(solution)/shard_map/all_to_all | solution.py:40
  148.5 0.0 all-gather.4.cloned.1.call-start
  148.6 9.2 %all-to-all-done = f32[128,1,24]{2,1,0:T(1,128)S(1)} async-done(((f32[128,1,24]{2,1,0:T(1,128)}), f32[128,1,24]{2,1,0:T(1,128)S(1)}, u32[]{:S(2)}, u32[]{:S(2)}) %all-to-all-start) | async-done | bytes 12320 | tf_op jit(solution)/shard_map/all_to_all | solution.py:40
  157.7 0.2 reduce_sum.87
  157.9 0.1 rsqrt_multiply_fusion
  158.0 0.1 rsqrt_multiply_fusion.1
  158.0 0.1 select_reduce_fusion.3
  158.2 0.1 select_reduce_fusion
  158.3 0.1 fusion.8
  158.5 0.9 maximum_bitcast_fusion
  159.4 0.5 copy-done.2
  159.9 2.0 multiply_subtract_fusion
  161.9 1.9 copy.53
  163.9 1.9 copy.54
  165.8 1.9 copy.55
  167.7 0.6 multiply_subtract_fusion.1
  168.3 59.7 %all-gather.4.cloned.1.call-done.i = bf16[16,51,4800]{2,1,0:T(8,128)(2,1)} async-done(((bf16[1,51,4800]{2,1,0:T(8,128)(2,1)}), bf16[16,51,4800]{2,1,0:T(8,128)(2,1)}) %all-gather.4.cloned.1.call-update) | async-done | bytes 7833616 | tf_op jit(solution)/shard_map/all_gather | solution.py:143
  228.0 1.3 slice_reduce_fusion
  229.3 0.8 reshape_squeeze.3
  230.1 5.9 %shard_map.180 = bf16[800,4800]{1,0:T(8,128)(2,1)} custom-call(bf16[16,51,4800]{2,1,0:T(8,128)(2,1)} %all-gather.4.cloned.1.call-done.i), custom_call_target="tpu_custom_call" | custom-call | tf_op jit(solution)/shard_map/pallas_call | solution.py:75
  (28 shorter events, 0.2 us)
Async XLA Ops:
  7.2 127.4 %reduce-scatter.4.cloned.1.call-start = ((), (), s32[]{:S(2)}) async-start(), calls=%async_computation.3 | async-start | bytes 18522112
  17.3 117.2 %copy-start.3 = (f32[1,1300]{1,0:T(1,128)S(1)}, f32[1,1300]{1,0:T(1,128)}, u32[]{:S(2)}) copy-start(f32[1,1300]{1,0:T(1,128)} %param.17) | copy-start | bytes 15604
  17.3 117.2 %copy-start.4 = (f32[1,1300]{1,0:T(1,128)S(1)}, f32[1,1300]{1,0:T(1,128)}, u32[]{:S(2)}) copy-start(f32[1,1300]{1,0:T(1,128)} %param.18) | copy-start | bytes 15604
  17.3 117.2 %copy-start.5 = (f32[1,1300]{1,0:T(1,128)S(1)}, f32[1,1300]{1,0:T(1,128)}, u32[]{:S(2)}) copy-start(f32[1,1300]{1,0:T(1,128)} %param.19) | copy-start | bytes 15604
  17.4 118.6 %copy-start.8 = (s32[8]{0:T(128)S(1)}, s32[8]{0:T(128)}, u32[]{:S(2)}) copy-start(s32[8]{0:T(128)} %constant.70.clone) | copy-start | bytes 100
  17.4 118.6 %copy-start.9 = (s32[8]{0:T(128)S(1)}, s32[8]{0:T(128)}, u32[]{:S(2)}) copy-start(s32[8]{0:T(128)} %constant.71.clone) | copy-start | bytes 100
  17.4 118.9 %copy-start = (f32[1,1,1,50,4800]{4,2,3,1,0:T(1,128)S(1)}, f32[1,1,1,50,4800]{4,2,3,1,0:T(1,128)}, u32[]{:S(2)}) copy-start(f32[1,1,1,50,4800]{4,2,3,1,0:T(1,128)} %param.14) | copy-start | bytes 2880004
  136.3 3.0 %copy-start.6 = (s32[4]{0:T(128)S(1)}, s32[4]{0:T(128)}, u32[]{:S(2)}) copy-start(s32[4]{0:T(128)} %constant.68.clone) | copy-start | bytes 52
  136.3 3.0 %copy-start.7 = (s32[4]{0:T(128)S(1)}, s32[4]{0:T(128)}, u32[]{:S(2)}) copy-start(s32[4]{0:T(128)} %constant.69.clone) | copy-start | bytes 52
  136.3 12.2 %copy-start.1 = (f32[1,51,4800]{2,1,0:T(8,128)S(1)}, f32[1,51,4800]{2,1,0:T(8,128)}, u32[]{:S(2)}) copy-start(f32[1,51,4800]{2,1,0:T(8,128)} %reduce-scatter.4.cloned.1.call-done) | copy-start | bytes 2937604
  140.4 17.4 %all-to-all-start = ((f32[128,1,24]{2,1,0:T(1,128)}), f32[128,1,24]{2,1,0:T(1,128)S(1)}, u32[]{:S(2)}, u32[]{:S(2)}) async-start(f32[128,1,24]{2,1,0:T(1,128)} %broadcast_in_dim.8), calls=%async_computation | async-start | bytes 131072 | tf_op jit(solution)/shard_map/all_to_all | solution.py:40
  148.5 79.6 %all-gather.4.cloned.1.call-start = ((), (), s32[]{:S(2)}) async-start(), calls=%async_computation.2 | async-start | bytes 9261056 | tf_op jit(solution)/shard_map/all_gather | solution.py:143
  158.5 1.4 copy-start.2
Sparse Core Ops, SparseCore 0:
  17.5 116.9 reduce-scatter.3
  159.5 68.4 all-gather.3

commit v8 on v7

--- a/solution.py
+++ b/solution.py
@@ -43,24 +43,24 @@
 def regroup_kernel(owned_rows, rows_ref, vec_ref, out_ref):
     for j in range(out_ref.shape[0]):
         out_ref[j, :owned_rows, :] = rows_ref[j * owned_rows : (j + 1) * owned_rows, :].astype(jnp.float32)
-        out_ref[j, owned_rows:, :] = vec_ref[j : j + 1, :]
+        out_ref[j, owned_rows:, :] = vec_ref[j]
 
 
 def regroup(rows, vec_rows, n_owners, owned_rows):
     columns = rows.shape[1]
-    per_step = 8
+    per_step = 4
     assert n_owners % per_step == 0
     return pl.pallas_call(
         lambda r, v, o: regroup_kernel(owned_rows, r, v, o),
         grid=(n_owners // per_step,),
         in_specs=[
             pl.BlockSpec((per_step * owned_rows, columns), lambda i: (i, 0)),
-            pl.BlockSpec((per_step, columns), lambda i: (i, 0)),
+            pl.BlockSpec((per_step, 1, columns), lambda i: (i, 0, 0)),
         ],
         out_specs=pl.BlockSpec((per_step, owned_rows + 1, columns), lambda i: (i, 0, 0)),
         out_shape=jax.ShapeDtypeStruct((n_owners, owned_rows + 1, columns), jnp.float32),
         compiler_params=pltpu.CompilerParams(vmem_limit_bytes=48 * 1024 * 1024),
-    )(rows, vec_rows)
+    )(rows, vec_rows.reshape(n_owners, 1, columns))
 
 
 def ungroup_kernel(owned_rows, in_ref, out_ref):
@@ -70,7 +70,7 @@
 
 def ungroup(gathered, owned_rows):
     n_owners, _, columns = gathered.shape
-    per_step = 8
+    per_step = 4
     assert n_owners % per_step == 0
     return pl.pallas_call(
         lambda i, o: ungroup_kernel(owned_rows, i, o),

time: 244 us -> 246 us (level)
  no operation moved by 1% of the time
where the time goes in v8:
time: 246 us; the launch traced here: 245 us
  waiting for transfers between devices  186 us (76%)
  Pallas kernels  16.6 us (7%)
  between operations  14.2 us (6%)
  other arithmetic  10.4 us (4%)
  local copies, waits for them, and re-layouts  9.47 us (4%)
  starting transfers between devices  8.18 us (3%)
    unnamed x3, waiting for transfers between devices  117 us
    all_gather x1, waiting for transfers between devices, local(): gathered = lax.all_gather(weights_rows, 'dp', axis=0, tiled=False)  59.7 us
    pallas_call x1, Pallas kernels, regroup(): pl.pallas_call(lambda r, v, o: regroup_kernel(owned_rows, r, v, o), grid=...  9.49 us
    all_to_all x1, waiting for transfers between devices, all_sum(): return jnp.sum(lax.all_to_all(copies, axes, 0, 0, tiled=True), axis=0)  9.17 us
    all_to_all x1, starting transfers between devices, all_sum(): return jnp.sum(lax.all_to_all(copies, axes, 0, 0, tiled=True), axis=0)  8.1 us
    pallas_call x1, Pallas kernels, ungroup(): pl.pallas_call(lambda i, o: ungroup_kernel(owned_rows, i, o), grid=(n_own...  7.12 us
    unnamed x23, local copies, waits for them, and re-layouts  6.37 us
  transfers between devices with their start and end apart: 3, of which 3 were waited for; matrix products, arithmetic and copies ran while one was open for 3% of the time, Pallas kernels for 0%

profile of v8, /device:TPU:0, one launch (start us, length us, event | category | flops | bytes accessed | tf_op | source)
XLA Modules:
  0.0 244.9 jit_solution(9112720958684110996)
XLA Ops:
  7.2 1.1 reduce.1
  8.3 0.1 convert_element_type.16
  8.5 0.2 reshape.159.v
  8.7 9.5 %shard_map.179 = f32[16,51,4800]{2,1,0:T(8,128)} custom-call(bf16[800,4800]{1,0:T(8,128)(2,1)} %bitcast.47, f32[16,1,4800]{2,1,0:T(1,128)S(1)} %reshape.159.v), custom_call_target="tpu_custom_call" | custom-call | tf_op jit(solution)/shard_map/pallas_call | solution.py:53
  18.3 117.1 %reduce-scatter.4.cloned.1.call-done = f32[1,51,4800]{2,1,0:T(8,128)} async-done(((f32[16,51,4800]{2,1,0:T(8,128)}), f32[1,51,4800]{2,1,0:T(8,128)}) %reduce-scatter.4.cloned.1.call-update) | async-done | bytes 979216
  135.4 1.4 multiply_reduce_fusion.1
  136.9 0.2 select_reduce_fusion.5
  137.1 0.1 broadcast_select_fusion
  137.2 3.0 %multiply_reduce_fusion = (f32[4800]{0:T(1024)S(1)}, f32[50,4800]{1,0:T(8,128)S(1)}, f32[4800]{0:T(1024)S(1)}) fusion(f32[1,1,1,50,4800]{4,2,3,1,0:T(1,128)S(1)} %copy-done, f32[1,1,1,50,4800]{4,2,3,1,0:T(1,128)} %param.16, f32[1,51,4800]{2,1,0:T(8,128)} %reduce-scatter.4.cloned.1.call-done, f32[1,1,1,50,4800]{4,2,3,1,0:T(1,128)} %param.15), kind=kLoop, calls=%fused_computation.22 | loop fusion | flops 4070400 | bytes 4838400 | tf_op jit(solution)/shard_map/reduce_sum | solution.py:124
  140.2 0.3 select_reduce_fusion.2
  140.5 0.1 pad_maximum_fusion
  140.6 0.7 broadcast_in_dim.8
  141.2 8.1 %all-to-all-start = ((f32[128,1,24]{2,1,0:T(1,128)}), f32[128,1,24]{2,1,0:T(1,128)S(1)}, u32[]{:S(2)}, u32[]{:S(2)}) async-start(f32[128,1,24]{2,1,0:T(1,128)} %broadcast_in_dim.8), calls=%async_computation | async-start | bytes 131072 | tf_op jit(solution)/shard_map/all_to_all | solution.py:40
  149.3 0.0 all-gather.4.cloned.1.call-start
  149.4 9.2 %all-to-all-done = f32[128,1,24]{2,1,0:T(1,128)S(1)} async-done(((f32[128,1,24]{2,1,0:T(1,128)}), f32[128,1,24]{2,1,0:T(1,128)S(1)}, u32[]{:S(2)}, u32[]{:S(2)}) %all-to-all-start) | async-done | bytes 12320 | tf_op jit(solution)/shard_map/all_to_all | solution.py:40
  158.6 0.2 reduce_sum.87
  158.8 0.1 rsqrt_multiply_fusion
  158.8 0.1 rsqrt_multiply_fusion.1
  158.9 0.1 select_reduce_fusion.3
  159.1 0.1 select_reduce_fusion
  159.2 0.1 fusion.8
  159.4 0.9 maximum_bitcast_fusion
  160.3 0.5 copy-done.2
  160.8 2.0 multiply_subtract_fusion
  162.8 1.9 copy.53
  164.7 1.9 copy.54
  166.7 1.9 copy.55
  168.6 0.6 multiply_subtract_fusion.1
  169.2 59.7 %all-gather.4.cloned.1.call-done.i = bf16[16,51,4800]{2,1,0:T(8,128)(2,1)} async-done(((bf16[1,51,4800]{2,1,0:T(8,128)(2,1)}), bf16[16,51,4800]{2,1,0:T(8,128)(2,1)}) %all-gather.4.cloned.1.call-update) | async-done | bytes 7833616 | tf_op jit(solution)/shard_map/all_gather | solution.py:143
  228.9 1.3 slice_reduce_fusion
  230.2 0.8 reshape_squeeze.3
  230.9 7.1 %shard_map.180 = bf16[800,4800]{1,0:T(8,128)(2,1)} custom-call(bf16[16,51,4800]{2,1,0:T(8,128)(2,1)} %all-gather.4.cloned.1.call-done.i), custom_call_target="tpu_custom_call" | custom-call | tf_op jit(solution)/shard_map/pallas_call | solution.py:75
  (29 shorter events, 0.2 us)
Async XLA Ops:
  7.2 128.2 %reduce-scatter.4.cloned.1.call-start = ((), (), s32[]{:S(2)}) async-start(), calls=%async_computation.3 | async-start | bytes 18522112
  18.2 117.2 %copy-start.3 = (f32[1,1300]{1,0:T(1,128)S(1)}, f32[1,1300]{1,0:T(1,128)}, u32[]{:S(2)}) copy-start(f32[1,1300]{1,0:T(1,128)} %param.17) | copy-start | bytes 15604
  18.2 117.2 %copy-start.4 = (f32[1,1300]{1,0:T(1,128)S(1)}, f32[1,1300]{1,0:T(1,128)}, u32[]{:S(2)}) copy-start(f32[1,1300]{1,0:T(1,128)} %param.18) | copy-start | bytes 15604
  18.2 117.2 %copy-start.5 = (f32[1,1300]{1,0:T(1,128)S(1)}, f32[1,1300]{1,0:T(1,128)}, u32[]{:S(2)}) copy-start(f32[1,1300]{1,0:T(1,128)} %param.19) | copy-start | bytes 15604
  18.2 118.6 %copy-start.8 = (s32[8]{0:T(128)S(1)}, s32[8]{0:T(128)}, u32[]{:S(2)}) copy-start(s32[8]{0:T(128)} %constant.70.clone) | copy-start | bytes 100
  18.2 118.6 %copy-start.9 = (s32[8]{0:T(128)S(1)}, s32[8]{0:T(128)}, u32[]{:S(2)}) copy-start(s32[8]{0:T(128)} %constant.71.clone) | copy-start | bytes 100
  18.2 118.9 %copy-start = (f32[1,1,1,50,4800]{4,2,3,1,0:T(1,128)S(1)}, f32[1,1,1,50,4800]{4,2,3,1,0:T(1,128)}, u32[]{:S(2)}) copy-start(f32[1,1,1,50,4800]{4,2,3,1,0:T(1,128)} %param.14) | copy-start | bytes 2880004
  137.2 3.0 %copy-start.6 = (s32[4]{0:T(128)S(1)}, s32[4]{0:T(128)}, u32[]{:S(2)}) copy-start(s32[4]{0:T(128)} %constant.68.clone) | copy-start | bytes 52
  137.2 3.0 %copy-start.7 = (s32[4]{0:T(128)S(1)}, s32[4]{0:T(128)}, u32[]{:S(2)}) copy-start(s32[4]{0:T(128)} %constant.69.clone) | copy-start | bytes 52
  137.2 12.2 %copy-start.1 = (f32[1,51,4800]{2,1,0:T(8,128)S(1)}, f32[1,51,4800]{2,1,0:T(8,128)}, u32[]{:S(2)}) copy-start(f32[1,51,4800]{2,1,0:T(8,128)} %reduce-scatter.4.cloned.1.call-done) | copy-start | bytes 2937604
  141.2 17.4 %all-to-all-start = ((f32[128,1,24]{2,1,0:T(1,128)}), f32[128,1,24]{2,1,0:T(1,128)S(1)}, u32[]{:S(2)}, u32[]{:S(2)}) async-start(f32[128,1,24]{2,1,0:T(1,128)} %broadcast_in_dim.8), calls=%async_computation | async-start | bytes 131072 | tf_op jit(solution)/shard_map/all_to_all | solution.py:40
  149.3 79.6 %all-gather.4.cloned.1.call-start = ((), (), s32[]{:S(2)}) async-start(), calls=%async_computation.2 | async-start | bytes 9261056 | tf_op jit(solution)/shard_map/all_gather | solution.py:143
  159.4 1.4 copy-start.2
Sparse Core Ops, SparseCore 0:
  18.4 116.9 reduce-scatter.3
  160.4 68.4 all-gather.3

commit v9 on v7

--- a/solution.py
+++ b/solution.py
@@ -63,21 +63,29 @@
     )(rows, vec_rows)
 
 
-def ungroup_kernel(owned_rows, in_ref, out_ref):
+def ungroup_kernel(owned_rows, in_ref, out_ref, vec_ref):
+    owned_vec = vec_ref.shape[2]
     for j in range(in_ref.shape[0]):
         out_ref[j * owned_rows : (j + 1) * owned_rows, :] = in_ref[j, :owned_rows, :]
+        vec_ref[j] = in_ref[j, owned_rows:, :owned_vec]
 
 
-def ungroup(gathered, owned_rows):
+def ungroup(gathered, owned_rows, owned_vec):
     n_owners, _, columns = gathered.shape
     per_step = 8
     assert n_owners % per_step == 0
     return pl.pallas_call(
-        lambda i, o: ungroup_kernel(owned_rows, i, o),
+        lambda i, o, v: ungroup_kernel(owned_rows, i, o, v),
         grid=(n_owners // per_step,),
         in_specs=[pl.BlockSpec((per_step, gathered.shape[1], columns), lambda i: (i, 0, 0))],
-        out_specs=pl.BlockSpec((per_step * owned_rows, columns), lambda i: (i, 0)),
-        out_shape=jax.ShapeDtypeStruct((n_owners * owned_rows, columns), gathered.dtype),
+        out_specs=[
+            pl.BlockSpec((per_step * owned_rows, columns), lambda i: (i, 0)),
+            pl.BlockSpec((per_step, 1, owned_vec), lambda i: (i, 0, 0)),
+        ],
+        out_shape=[
+            jax.ShapeDtypeStruct((n_owners * owned_rows, columns), gathered.dtype),
+            jax.ShapeDtypeStruct((n_owners, 1, owned_vec), gathered.dtype),
+        ],
         compiler_params=pltpu.CompilerParams(vmem_limit_bytes=48 * 1024 * 1024),
     )(gathered)
 
@@ -141,8 +149,9 @@
     weights_v_row = jnp.pad(master_v_new.astype(jnp.bfloat16), (0, columns - owned_vec))[None, :]
     weights_rows = jnp.concatenate([master_new.astype(jnp.bfloat16), weights_v_row], axis=0)
     gathered = lax.all_gather(weights_rows, "dp", axis=0, tiled=False)
-    weights_mat = ungroup(gathered, owned_rows).reshape(1, section_rows, columns)
-    weights_vec = gathered[:, owned_rows, :owned_vec].reshape(vec_length)
+    weights_rows, weights_v_rows = ungroup(gathered, owned_rows, owned_vec)
+    weights_mat = weights_rows.reshape(1, section_rows, columns)
+    weights_vec = weights_v_rows.reshape(vec_length)
     return (
         weights_mat,
         weights_vec,

time: 244 us -> 243 us (level)
  transfers between devices with their start and end apart: 3 -> 3, of which waited for: 3 -> 3; matrix products, arithmetic and copies ran while one was open for 3% -> 4% of each run, Pallas kernels for 0% -> 0%
where the time goes in v9:
time: 243 us; the launch traced here: 242 us
  waiting for transfers between devices  186 us (77%)
  Pallas kernels  14.8 us (6%)
  between operations  14.2 us (6%)
  other arithmetic  10.7 us (4%)
  starting transfers between devices  8.18 us (3%)
  local copies, waits for them, and re-layouts  7.99 us (3%)
    unnamed x3, waiting for transfers between devices  117 us
    all_gather x1, waiting for transfers between devices, local(): gathered = lax.all_gather(weights_rows, 'dp', axis=0, tiled=False)  59.7 us
    all_to_all x1, waiting for transfers between devices, all_sum(): return jnp.sum(lax.all_to_all(copies, axes, 0, 0, tiled=True), axis=0)  9.17 us
    pallas_call x1, Pallas kernels, regroup(): pl.pallas_call(lambda r, v, o: regroup_kernel(owned_rows, r, v, o), grid=...  8.84 us
    all_to_all x1, starting transfers between devices, all_sum(): return jnp.sum(lax.all_to_all(copies, axes, 0, 0, tiled=True), axis=0)  8.1 us
    unnamed x23, local copies, waits for them, and re-layouts  6.37 us
    pallas_call x1, Pallas kernels, ungroup(): pl.pallas_call(lambda i, o, v: ungroup_kernel(owned_rows, i, o, v), grid=...  5.95 us
  transfers between devices with their start and end apart: 3, of which 3 were waited for; matrix products, arithmetic and copies ran while one was open for 4% of the time, Pallas kernels for 0%

profile of v9, /device:TPU:0, one launch (start us, length us, event | category | flops | bytes accessed | tf_op | source)
XLA Modules:
  0.0 241.8 jit_solution(13067256034337133567)
XLA Ops:
  7.2 0.0 reduce-scatter.4.cloned.1.call-start
  7.2 1.1 reduce.1
  8.3 0.1 convert_element_type.16
  8.5 8.8 %shard_map.179 = f32[16,51,4800]{2,1,0:T(8,128)} custom-call(bf16[800,4800]{1,0:T(8,128)(2,1)} %bitcast.46, f32[16,4800]{1,0:T(8,128)S(1)} %pad_convert_fusion.v), custom_call_target="tpu_custom_call" | custom-call | tf_op jit(solution)/shard_map/pallas_call | solution.py:53
  17.4 117.1 %reduce-scatter.4.cloned.1.call-done = f32[1,51,4800]{2,1,0:T(8,128)} async-done(((f32[16,51,4800]{2,1,0:T(8,128)}), f32[1,51,4800]{2,1,0:T(8,128)}) %reduce-scatter.4.cloned.1.call-update) | async-done | bytes 979216
  134.5 1.4 multiply_reduce_fusion.1
  136.0 0.2 select_reduce_fusion.5
  136.2 0.1 broadcast_select_fusion
  136.3 3.0 %multiply_reduce_fusion = (f32[4800]{0:T(1024)S(1)}, f32[50,4800]{1,0:T(8,128)S(1)}, f32[4800]{0:T(1024)S(1)}) fusion(f32[1,1,1,50,4800]{4,2,3,1,0:T(1,128)S(1)} %copy-done, f32[1,1,1,50,4800]{4,2,3,1,0:T(1,128)} %param.16, f32[1,51,4800]{2,1,0:T(8,128)} %reduce-scatter.4.cloned.1.call-done, f32[1,1,1,50,4800]{4,2,3,1,0:T(1,128)} %param.15), kind=kLoop, calls=%fused_computation.22 | loop fusion | flops 4070400 | bytes 4838400 | tf_op jit(solution)/shard_map/reduce_sum | solution.py:132
  139.3 0.3 select_reduce_fusion.2
  139.6 0.1 pad_maximum_fusion
  139.7 0.7 broadcast_in_dim.8
  140.4 8.1 %all-to-all-start = ((f32[128,1,24]{2,1,0:T(1,128)}), f32[128,1,24]{2,1,0:T(1,128)S(1)}, u32[]{:S(2)}, u32[]{:S(2)}) async-start(f32[128,1,24]{2,1,0:T(1,128)} %broadcast_in_dim.8), calls=%async_computation | async-start | bytes 131072 | tf_op jit(solution)/shard_map/all_to_all | solution.py:40
  148.5 0.0 all-gather.4.cloned.1.call-start
  148.6 9.2 %all-to-all-done = f32[128,1,24]{2,1,0:T(1,128)S(1)} async-done(((f32[128,1,24]{2,1,0:T(1,128)}), f32[128,1,24]{2,1,0:T(1,128)S(1)}, u32[]{:S(2)}, u32[]{:S(2)}) %all-to-all-start) | async-done | bytes 12320 | tf_op jit(solution)/shard_map/all_to_all | solution.py:40
  157.7 0.2 reduce_sum.87
  157.9 0.1 rsqrt_multiply_fusion
  158.0 0.1 rsqrt_multiply_fusion.1
  158.0 0.1 select_reduce_fusion.3
  158.2 0.1 select_reduce_fusion
  158.3 0.1 fusion.8
  158.5 0.9 maximum_bitcast_fusion
  159.4 0.5 copy-done.2
  159.9 2.0 multiply_subtract_fusion
  161.9 1.9 copy.53
  163.8 1.9 copy.54
  165.8 1.9 copy.55
  167.7 0.6 multiply_subtract_fusion.1
  168.3 59.7 %all-gather.4.cloned.1.call-done.i = bf16[16,51,4800]{2,1,0:T(8,128)(2,1)} async-done(((bf16[1,51,4800]{2,1,0:T(8,128)(2,1)}), bf16[16,51,4800]{2,1,0:T(8,128)(2,1)}) %all-gather.4.cloned.1.call-update) | async-done | bytes 7833616 | tf_op jit(solution)/shard_map/all_gather | solution.py:151
  228.0 5.9 %shard_map.180 = (bf16[800,4800]{1,0:T(8,128)(2,1)}, bf16[16,1,1300]{2,1,0:T(2,128)(2,1)S(1)}) custom-call(bf16[16,51,4800]{2,1,0:T(8,128)(2,1)} %all-gather.4.cloned.1.call-done.i), custom_call_target="tpu_custom_call" | custom-call | tf_op jit(solution)/shard_map/pallas_call | solution.py:77
  234.0 0.3 reduce.8
  234.2 0.8 reshape.154
  (28 shorter events, 0.2 us)
Async XLA Ops:
  7.2 127.4 %reduce-scatter.4.cloned.1.call-start = ((), (), s32[]{:S(2)}) async-start(), calls=%async_computation.3 | async-start | bytes 18522112
  17.3 117.2 %copy-start.3 = (f32[1,1300]{1,0:T(1,128)S(1)}, f32[1,1300]{1,0:T(1,128)}, u32[]{:S(2)}) copy-start(f32[1,1300]{1,0:T(1,128)} %param.17) | copy-start | bytes 15604
  17.3 117.2 %copy-start.4 = (f32[1,1300]{1,0:T(1,128)S(1)}, f32[1,1300]{1,0:T(1,128)}, u32[]{:S(2)}) copy-start(f32[1,1300]{1,0:T(1,128)} %param.18) | copy-start | bytes 15604
  17.3 117.2 %copy-start.5 = (f32[1,1300]{1,0:T(1,128)S(1)}, f32[1,1300]{1,0:T(1,128)}, u32[]{:S(2)}) copy-start(f32[1,1300]{1,0:T(1,128)} %param.19) | copy-start | bytes 15604
  17.4 118.6 %copy-start.8 = (s32[8]{0:T(128)S(1)}, s32[8]{0:T(128)}, u32[]{:S(2)}) copy-start(s32[8]{0:T(128)} %constant.70.clone) | copy-start | bytes 100
  17.4 118.6 %copy-start.9 = (s32[8]{0:T(128)S(1)}, s32[8]{0:T(128)}, u32[]{:S(2)}) copy-start(s32[8]{0:T(128)} %constant.71.clone) | copy-start | bytes 100
  17.4 118.9 %copy-start = (f32[1,1,1,50,4800]{4,2,3,1,0:T(1,128)S(1)}, f32[1,1,1,50,4800]{4,2,3,1,0:T(1,128)}, u32[]{:S(2)}) copy-start(f32[1,1,1,50,4800]{4,2,3,1,0:T(1,128)} %param.14) | copy-start | bytes 2880004
  136.3 3.0 %copy-start.6 = (s32[4]{0:T(128)S(1)}, s32[4]{0:T(128)}, u32[]{:S(2)}) copy-start(s32[4]{0:T(128)} %constant.68.clone) | copy-start | bytes 52
  136.3 3.0 %copy-start.7 = (s32[4]{0:T(128)S(1)}, s32[4]{0:T(128)}, u32[]{:S(2)}) copy-start(s32[4]{0:T(128)} %constant.69.clone) | copy-start | bytes 52
  136.3 12.2 %copy-start.1 = (f32[1,51,4800]{2,1,0:T(8,128)S(1)}, f32[1,51,4800]{2,1,0:T(8,128)}, u32[]{:S(2)}) copy-start(f32[1,51,4800]{2,1,0:T(8,128)} %reduce-scatter.4.cloned.1.call-done) | copy-start | bytes 2937604
  140.4 17.4 %all-to-all-start = ((f32[128,1,24]{2,1,0:T(1,128)}), f32[128,1,24]{2,1,0:T(1,128)S(1)}, u32[]{:S(2)}, u32[]{:S(2)}) async-start(f32[128,1,24]{2,1,0:T(1,128)} %broadcast_in_dim.8), calls=%async_computation | async-start | bytes 131072 | tf_op jit(solution)/shard_map/all_to_all | solution.py:40
  148.5 79.6 %all-gather.4.cloned.1.call-start = ((), (), s32[]{:S(2)}) async-start(), calls=%async_computation.2 | async-start | bytes 9261056 | tf_op jit(solution)/shard_map/all_gather | solution.py:151
  158.5 1.4 copy-start.2
Sparse Core Ops, SparseCore 0:
  17.5 116.9 reduce-scatter.3
  159.5 68.4 all-gather.3

commit v10 on v9

--- a/solution.py
+++ b/solution.py
@@ -40,27 +40,35 @@
     return jnp.sum(lax.all_to_all(copies, axes, 0, 0, tiled=True), axis=0)
 
 
-def regroup_kernel(owned_rows, rows_ref, vec_ref, out_ref):
-    for j in range(out_ref.shape[0]):
+def regroup_kernel(owned_rows, owned_vec, rows_ref, vec_ref, out_ref):
+    per_step = out_ref.shape[0]
+    for j in range(per_step):
         out_ref[j, :owned_rows, :] = rows_ref[j * owned_rows : (j + 1) * owned_rows, :].astype(jnp.float32)
-        out_ref[j, owned_rows:, :] = vec_ref[j : j + 1, :]
+        out_ref[j, owned_rows:, :] = jnp.zeros((1, out_ref.shape[2]), jnp.float32)
+    for step in range(2):
+        @pl.when(pl.program_id(0) == step)
+        def _():
+            for j in range(per_step):
+                owner = step * per_step + j
+                out_ref[j, owned_rows:, :owned_vec] = vec_ref[:, owner * owned_vec : (owner + 1) * owned_vec].astype(jnp.float32)
 
 
-def regroup(rows, vec_rows, n_owners, owned_rows):
+def regroup(rows, vec, n_owners, owned_rows):
     columns = rows.shape[1]
+    owned_vec = vec.shape[1] // n_owners
     per_step = 8
-    assert n_owners % per_step == 0
+    assert n_owners == 2 * per_step
     return pl.pallas_call(
-        lambda r, v, o: regroup_kernel(owned_rows, r, v, o),
+        lambda r, v, o: regroup_kernel(owned_rows, owned_vec, r, v, o),
         grid=(n_owners // per_step,),
         in_specs=[
             pl.BlockSpec((per_step * owned_rows, columns), lambda i: (i, 0)),
-            pl.BlockSpec((per_step, columns), lambda i: (i, 0)),
+            pl.BlockSpec((1, vec.shape[1]), lambda i: (0, 0)),
         ],
         out_specs=pl.BlockSpec((per_step, owned_rows + 1, columns), lambda i: (i, 0, 0)),
         out_shape=jax.ShapeDtypeStruct((n_owners, owned_rows + 1, columns), jnp.float32),
         compiler_params=pltpu.CompilerParams(vmem_limit_bytes=48 * 1024 * 1024),
-    )(rows, vec_rows)
+    )(rows, vec)
 
 
 def ungroup_kernel(owned_rows, in_ref, out_ref, vec_ref):
@@ -115,8 +123,7 @@
     vec_index = lax.axis_index("dp") * owned_vec + lax.iota(jnp.int32, owned_vec)
     masks_vec = segment_masks(vec_index, bounds_vec)
 
-    local_vec = jnp.pad(grad_vec.reshape(n_dp, owned_vec).astype(jnp.float32), ((0, 0), (0, columns - owned_vec)))
-    payload = regroup(grad_mat.reshape(section_rows, columns), local_vec, n_dp, owned_rows)
+    payload = regroup(grad_mat.reshape(section_rows, columns), grad_vec, n_dp, owned_rows)
     summed = lax.optimization_barrier(lax.psum_scatter(payload, "dp", scatter_dimension=0, tiled=True))
     gradient = summed[0, :owned_rows]
     gradient_v = summed[0, owned_rows, :owned_vec]

time: 243 us -> 242 us (level)
    unnamed x23 -> x25, local copies, waits for them, and re-layouts: 6.37 us -> 7.25 us
where the time goes in v10:
time: 242 us
  waiting for transfers between devices  186 us (77%)
  Pallas kernels  14.9 us (6%)
  between operations  14.2 us (6%)
  other arithmetic  9.52 us (4%)
  local copies, waits for them, and re-layouts  8.73 us (4%)
  starting transfers between devices  8.18 us (3%)
    unnamed x3, waiting for transfers between devices  117 us
    all_gather x1, waiting for transfers between devices, local(): gathered = lax.all_gather(weights_rows, 'dp', axis=0, tiled=False)  59.7 us
    all_to_all x1, waiting for transfers between devices, all_sum(): return jnp.sum(lax.all_to_all(copies, axes, 0, 0, tiled=True), axis=0)  9.17 us
    pallas_call x1, Pallas kernels, regroup(): pl.pallas_call(lambda r, v, o: regroup_kernel(owned_rows, owned_vec, r, v...  8.91 us
    all_to_all x1, starting transfers between devices, all_sum(): return jnp.sum(lax.all_to_all(copies, axes, 0, 0, tiled=True), axis=0)  8.1 us
    unnamed x25, local copies, waits for them, and re-layouts  7.25 us
    pallas_call x1, Pallas kernels, ungroup(): pl.pallas_call(lambda i, o, v: ungroup_kernel(owned_rows, i, o, v), grid=...  5.95 us
  transfers between devices with their start and end apart: 3, of which 3 were waited for; matrix products, arithmetic and copies ran while one was open for 4% of the time, Pallas kernels for 0%

profile of v10, /device:TPU:0, one launch (start us, length us, event | category | flops | bytes accessed | tf_op | source)
XLA Modules:
  0.0 241.5 jit_solution(6357817316288086327)
XLA Ops:
  7.2 0.0 reduce-scatter.4.cloned.1.call-start
  7.2 0.9 copy-done
  8.1 8.9 %shard_map.179 = f32[16,51,4800]{2,1,0:T(8,128)} custom-call(bf16[800,4800]{1,0:T(8,128)(2,1)} %bitcast.46, bf16[1,20800]{1,0:T(2,128)(2,1)S(1)} %copy-done), custom_call_target="tpu_custom_call" | custom-call | tf_op jit(solution)/shard_map/pallas_call | solution.py:61
  17.0 0.0 reduce-scatter.4.cloned.1.call-update
  17.1 117.1 %reduce-scatter.4.cloned.1.call-done = f32[1,51,4800]{2,1,0:T(8,128)} async-done(((f32[16,51,4800]{2,1,0:T(8,128)}), f32[1,51,4800]{2,1,0:T(8,128)}) %reduce-scatter.4.cloned.1.call-update) | async-done | bytes 979216
  134.2 1.4 multiply_reduce_fusion.1
  135.7 0.2 select_reduce_fusion.5
  135.9 0.1 broadcast_select_fusion
  136.0 3.0 %multiply_reduce_fusion = (f32[4800]{0:T(1024)S(1)}, f32[50,4800]{1,0:T(8,128)S(1)}, f32[4800]{0:T(1024)S(1)}) fusion(f32[1,1,1,50,4800]{4,2,3,1,0:T(1,128)S(1)} %copy-done.1, f32[1,1,1,50,4800]{4,2,3,1,0:T(1,128)} %param.16, f32[1,51,4800]{2,1,0:T(8,128)} %reduce-scatter.4.cloned.1.call-done, f32[1,1,1,50,4800]{4,2,3,1,0:T(1,128)} %param.15), kind=kLoop, calls=%fused_computation.22 | loop fusion | flops 4070400 | bytes 4838400 | tf_op jit(solution)/shard_map/reduce_sum | solution.py:139
  139.0 0.3 select_reduce_fusion.2
  139.3 0.1 pad_maximum_fusion
  139.3 0.7 broadcast_in_dim.8
  140.0 8.1 %all-to-all-start = ((f32[128,1,24]{2,1,0:T(1,128)}), f32[128,1,24]{2,1,0:T(1,128)S(1)}, u32[]{:S(2)}, u32[]{:S(2)}) async-start(f32[128,1,24]{2,1,0:T(1,128)} %broadcast_in_dim.8), calls=%async_computation | async-start | bytes 131072 | tf_op jit(solution)/shard_map/all_to_all | solution.py:40
  148.1 0.0 all-gather.4.cloned.1.call-start
  148.2 9.2 %all-to-all-done = f32[128,1,24]{2,1,0:T(1,128)S(1)} async-done(((f32[128,1,24]{2,1,0:T(1,128)}), f32[128,1,24]{2,1,0:T(1,128)S(1)}, u32[]{:S(2)}, u32[]{:S(2)}) %all-to-all-start) | async-done | bytes 12320 | tf_op jit(solution)/shard_map/all_to_all | solution.py:40
  157.4 0.2 reduce_sum.87
  157.5 0.1 rsqrt_multiply_fusion
  157.6 0.1 rsqrt_multiply_fusion.1
  157.7 0.1 select_reduce_fusion.3
  157.9 0.1 select_reduce_fusion
  158.0 0.1 fusion.8
  158.2 0.9 maximum_bitcast_fusion
  159.0 0.5 copy-done.3
  159.5 2.0 multiply_subtract_fusion
  161.6 1.9 copy.53
  163.5 1.9 copy.54
  165.5 1.9 copy.55
  167.4 0.6 multiply_subtract_fusion.1
  168.0 59.7 %all-gather.4.cloned.1.call-done.i = bf16[16,51,4800]{2,1,0:T(8,128)(2,1)} async-done(((bf16[1,51,4800]{2,1,0:T(8,128)(2,1)}), bf16[16,51,4800]{2,1,0:T(8,128)(2,1)}) %all-gather.4.cloned.1.call-update) | async-done | bytes 7833616 | tf_op jit(solution)/shard_map/all_gather | solution.py:158
  227.7 5.9 %shard_map.180 = (bf16[800,4800]{1,0:T(8,128)(2,1)}, bf16[16,1,1300]{2,1,0:T(2,128)(2,1)S(1)}) custom-call(bf16[16,51,4800]{2,1,0:T(8,128)(2,1)} %all-gather.4.cloned.1.call-done.i), custom_call_target="tpu_custom_call" | custom-call | tf_op jit(solution)/shard_map/pallas_call | solution.py:85
  233.7 0.3 reduce.7
  233.9 0.8 reshape.151
  (27 shorter events, 0.1 us)
Async XLA Ops:
  7.2 127.0 %reduce-scatter.4.cloned.1.call-start = ((), (), s32[]{:S(2)}) async-start(), calls=%async_computation.3 | async-start | bytes 18522112
  7.2 0.9 copy-start
  17.0 117.2 %copy-start.4 = (f32[1,1300]{1,0:T(1,128)S(1)}, f32[1,1300]{1,0:T(1,128)}, u32[]{:S(2)}) copy-start(f32[1,1300]{1,0:T(1,128)} %param.17) | copy-start | bytes 15604
  17.0 117.2 %copy-start.5 = (f32[1,1300]{1,0:T(1,128)S(1)}, f32[1,1300]{1,0:T(1,128)}, u32[]{:S(2)}) copy-start(f32[1,1300]{1,0:T(1,128)} %param.18) | copy-start | bytes 15604
  17.0 117.2 %copy-start.6 = (f32[1,1300]{1,0:T(1,128)S(1)}, f32[1,1300]{1,0:T(1,128)}, u32[]{:S(2)}) copy-start(f32[1,1300]{1,0:T(1,128)} %param.19) | copy-start | bytes 15604
  17.0 118.6 %copy-start.9 = (s32[8]{0:T(128)S(1)}, s32[8]{0:T(128)}, u32[]{:S(2)}) copy-start(s32[8]{0:T(128)} %constant.68.clone) | copy-start | bytes 100
  17.0 118.6 %copy-start.10 = (s32[8]{0:T(128)S(1)}, s32[8]{0:T(128)}, u32[]{:S(2)}) copy-start(s32[8]{0:T(128)} %constant.69.clone) | copy-start | bytes 100
  17.0 118.9 %copy-start.1 = (f32[1,1,1,50,4800]{4,2,3,1,0:T(1,128)S(1)}, f32[1,1,1,50,4800]{4,2,3,1,0:T(1,128)}, u32[]{:S(2)}) copy-start(f32[1,1,1,50,4800]{4,2,3,1,0:T(1,128)} %param.14) | copy-start | bytes 2880004
  136.0 3.0 %copy-start.7 = (s32[4]{0:T(128)S(1)}, s32[4]{0:T(128)}, u32[]{:S(2)}) copy-start(s32[4]{0:T(128)} %constant.66.clone) | copy-start | bytes 52
  136.0 3.0 %copy-start.8 = (s32[4]{0:T(128)S(1)}, s32[4]{0:T(128)}, u32[]{:S(2)}) copy-start(s32[4]{0:T(128)} %constant.67.clone) | copy-start | bytes 52
  136.0 12.2 %copy-start.2 = (f32[1,51,4800]{2,1,0:T(8,128)S(1)}, f32[1,51,4800]{2,1,0:T(8,128)}, u32[]{:S(2)}) copy-start(f32[1,51,4800]{2,1,0:T(8,128)} %reduce-scatter.4.cloned.1.call-done) | copy-start | bytes 2937604
  140.0 17.4 %all-to-all-start = ((f32[128,1,24]{2,1,0:T(1,128)}), f32[128,1,24]{2,1,0:T(1,128)S(1)}, u32[]{:S(2)}, u32[]{:S(2)}) async-start(f32[128,1,24]{2,1,0:T(1,128)} %broadcast_in_dim.8), calls=%async_computation | async-start | bytes 131072 | tf_op jit(solution)/shard_map/all_to_all | solution.py:40
  148.1 79.6 %all-gather.4.cloned.1.call-start = ((), (), s32[]{:S(2)}) async-start(), calls=%async_computation.2 | async-start | bytes 9261056 | tf_op jit(solution)/shard_map/all_gather | solution.py:158
  158.1 1.4 copy-start.3
Sparse Core Ops, SparseCore 0:
  17.2 116.9 reduce-scatter.3
  159.2 68.4 all-gather.3
